TPU v7x, 256 devices: a whole 4x4x8 slice. The times are simulated.
256 devices in a mesh: seq: 32 (over x, z_lo, core), mp: 8 (over y, z_hi).
Axes of the slice: x: 4, y: 4, z: 8 (z_hi: 2, z_lo: 4; z = z_hi * 4 + z_lo), core: 2. Of those that a mesh axis runs over, the one named last changes fastest.
Arguments:
- tokens: bfloat16 [8192, 4096], P('seq', 'mp'), may hold values from -6 to 6
- norm_gain: bfloat16 [4096], replicated, may hold values from 0.5 to 1.5
- norm_bias: bfloat16 [4096], replicated, may hold values from -4 to 4
- w_query: bfloat16 [4096, 2048], P(None, 'mp'), may hold values from -0.25 to 0.25
- w_keyval: bfloat16 [4096, 2, 2048], P(None, None, 'mp'), may hold values from -0.09375 to 0.09375
- w_out: bfloat16 [2048, 4096], P('mp'), may hold values from -0.125 to 0.125
- prefix_key: bfloat16 [8192, 2048], P('seq', 'mp'), may hold values from -82 to 82
- prefix_value: bfloat16 [8192, 2048], P('seq', 'mp'), may hold values from -6 to 6
- lengths: int32 [16], replicated, may hold values from 1 to 1024, 8192 in all
- context: int32 [16], replicated, may hold values from 256 to 8192
- prefix_place: int32 [64], replicated, may hold values from 0 to 63, each once
Outputs:
- attn_out: bfloat16 [8192, 4096], P(('seq', 'mp'))
Inputs may be any that keep to these rules, and one draw needn't show every extreme that they name: The lengths add up to 8192, and one request has exactly 1024 tokens. Stored block j holds the prefix positions prefix_place[j] * 128 to prefix_place[j] * 128 + 127; every block appears once.
All inputs are finite; a program needn't handle non-finite values.
Results may differ from a plain program's by a relative error of at most 0.02.
The roundings to bfloat16 on the way count: a program that leaves them out, or rounds other values in their place, can miss the bound.
Values may be sent and summed in bfloat16 or wider, within the bound.
No kernel may reach another device: no remote copies, remote signals or barrier semaphores. Data moves between devices by JAX's collectives and lax.ppermute only.
A program may use at most 128 MiB of HBM per device.

v0:
```python
import math

import jax
import jax.numpy as jnp
from jax import lax
from jax.sharding import PartitionSpec as P

HD = 128
PBLOCK = 128


NEG_FILL = -1e30


def layer_norm(rows_in, norm_gain, norm_bias):
    as_float = rows_in.astype(jnp.float32)
    row_mean = jnp.mean(as_float, -1, keepdims=True)
    centered = as_float - row_mean
    row_var = jnp.mean(centered * centered, -1, keepdims=True)
    scaled = centered * lax.rsqrt(row_var + 1e-05)
    return (scaled * norm_gain.astype(jnp.float32) + norm_bias.astype(jnp.float32)).astype(
        jnp.bfloat16
    )


def rotate(column_block, position):
    head_dim = column_block.shape[-1]
    half_rot = head_dim // 8
    inverse_freq = jnp.power(
        jnp.float32(10000.0), -jnp.arange(half_rot, dtype=jnp.float32) * (8.0 / head_dim)
    )
    angles = position.astype(jnp.float32)[:, None] * inverse_freq[None, :]
    cosine = jnp.cos(angles)[:, None, :]
    sines = jnp.sin(angles)[:, None, :]
    first_half = column_block[..., :half_rot]
    second = column_block[..., half_rot : 2 * half_rot]
    return jnp.concatenate(
        [
            first_half * cosine - second * sines,
            second * cosine + first_half * sines,
            column_block[..., 2 * half_rot :],
        ],
        -1,
    )


def request_info(global_index, lengths, context):
    request_end = jnp.cumsum(lengths)
    starts = request_end - lengths
    inside = (
        (global_index[:, None] >= starts[None, :]) & (global_index[:, None] < request_end[None, :])
    ).astype(jnp.int32)
    labels = jnp.arange(lengths.shape[0], dtype=jnp.int32) + 1
    request = jnp.sum(inside * labels[None, :], 1) - 1
    cached_len = jnp.sum(inside * context[None, :], 1)
    position = jnp.sum(inside * (context - starts)[None, :], 1) + global_index
    return (request, cached_len, position)


def attend(running, queries, key_rows, values, visible):
    row_max, row_sum, weighted = running
    scores = jnp.einsum("qhd,khd->qhk", queries, key_rows, preferred_element_type=jnp.float32) * (
        1.0 / math.sqrt(queries.shape[-1])
    )
    visible_wide = visible[:, None, :]
    new_max = jnp.maximum(row_max, jnp.max(jnp.where(visible_wide, scores, NEG_FILL), -1))
    factor = jnp.exp(row_max - new_max)
    exp_terms = jnp.where(visible_wide, jnp.exp(scores - new_max[..., None]), 0.0)
    row_sum = row_sum * factor + jnp.sum(exp_terms, -1)
    weighted = weighted * factor[..., None] + jnp.einsum(
        "qhk,khd->qhd", exp_terms.astype(jnp.bfloat16), values, preferred_element_type=jnp.float32
    )
    return (new_max, row_sum, weighted)


def fold_block(running, queries, key_rows, values, visible):
    return attend(running, queries, key_rows, values, visible)


def body(
    tokens,
    norm_gain,
    norm_bias,
    w_query,
    w_keyval,
    w_out,
    prefix_key,
    prefix_value,
    lengths,
    context,
    prefix_place,
):
    gathered = lax.all_gather(tokens, "mp", axis=1, tiled=True)
    token_count = gathered.shape[0]
    feature_count = gathered.shape[1]
    local_heads = w_query.shape[1] // HD
    normed = layer_norm(gathered, norm_gain, norm_bias)
    seq_index = lax.axis_index("seq")
    global_index = seq_index * token_count + jnp.arange(token_count, dtype=jnp.int32)
    request, cached_len, position = request_info(global_index, lengths, context)
    query_raw = jnp.dot(normed, w_query, preferred_element_type=jnp.float32).reshape(
        token_count, local_heads, HD
    )
    key_value_raw = jnp.dot(
        normed, w_keyval.reshape(feature_count, -1), preferred_element_type=jnp.float32
    ).reshape(token_count, 2, local_heads, HD)
    queries = rotate(query_raw, position).astype(jnp.bfloat16)
    own_keys = rotate(key_value_raw[:, 0], position).astype(jnp.bfloat16)
    own_values = key_value_raw[:, 1].astype(jnp.bfloat16)
    key_value = jnp.stack([own_keys, own_values], 1)
    prefix_rows = prefix_key.shape[0]
    prefix_keys = prefix_key.reshape(1, prefix_rows, local_heads, HD)
    prefix_values = prefix_value.reshape(1, prefix_rows, local_heads, HD)
    start_state = (
        jnp.full((token_count, local_heads), NEG_FILL, jnp.float32),
        jnp.zeros((token_count, local_heads), jnp.float32),
        jnp.zeros((token_count, local_heads, HD), jnp.float32),
    )

    def suffix_visible(source):
        key_index = source * token_count + jnp.arange(token_count, dtype=jnp.int32)
        key_request = request_info(key_index, lengths, context)[0]
        return (key_request[None, :] == request[:, None]) & (
            key_index[None, :] <= global_index[:, None]
        )

    def prefix_visible(source):
        per_device = prefix_rows // PBLOCK
        blocks = lax.dynamic_slice_in_dim(prefix_place, source * per_device, per_device, 0)
        logical = (blocks[:, None] * PBLOCK + jnp.arange(PBLOCK, dtype=jnp.int32)[None, :]).reshape(
            -1
        )
        return logical[None, :] < cached_len[:, None]

    pieces = (
        lax.all_gather(key_value[None], "seq", axis=0, tiled=True),
        lax.all_gather(prefix_keys, "seq", axis=0, tiled=True),
        lax.all_gather(prefix_values, "seq", axis=0, tiled=True),
    )

    def scan_step(state_now, scan_item):
        source, pair_block, key_block, value_block = scan_item
        state_now = fold_block(state_now, queries, key_block, value_block, prefix_visible(source))
        state_now = fold_block(
            state_now, queries, pair_block[:, 0], pair_block[:, 1], suffix_visible(source)
        )
        return (state_now, None)

    shard_count = pieces[0].shape[0]
    sources = jnp.arange(shard_count, dtype=jnp.int32)
    row_max, row_sum, weighted = lax.scan(
        scan_step, start_state, (sources, pieces[0], pieces[1], pieces[2])
    )[0]
    heads_out = (
        (weighted / row_sum[..., None]).astype(jnp.bfloat16).reshape(token_count, local_heads * HD)
    )
    summed = lax.psum_scatter(
        jnp.dot(heads_out, w_out, preferred_element_type=jnp.float32).astype(jnp.bfloat16),
        "mp",
        scatter_dimension=0,
        tiled=True,
    )
    return summed


def solution(mesh):
    return jax.shard_map(
        body,
        mesh=mesh,
        in_specs=(
            P("seq", "mp"),
            P(),
            P(),
            P(None, "mp"),
            P(None, None, "mp"),
            P("mp", None),
            P("seq", "mp"),
            P("seq", "mp"),
            P(),
            P(),
            P(),
        ),
        out_specs=P(("seq", "mp"), None),
        check_vma=False,
    )
```

profile of v0, /device:TPU:2, one launch (start us, length us, event | category | flops | bytes accessed | tf_op | source)
XLA Modules:
  0.0 766.5 jit_solution(576834469604589329)
XLA Ops:
  9.6 4.9 copy.74
  14.5 6.4 copy.62
  23.0 65.4 %all-gather.8.cloned.1.call-done = bf16[256,4096]{1,0:T(8,128)(2,1)} async-done(((bf16[256,512]{1,0:T(8,128)(2,1)}), bf16[256,4096]{1,0:T(8,128)(2,1)}) %all-gather.8.cloned.1.call-update) | async-done | bytes 2097168 | tf_op jit(solution)/shard_map/all_gather | solution.py:93
  88.4 2.1 convert_reduce_fusion
  90.5 2.3 fusion.33
  92.8 3.8 fusion.37
  96.8 1.4 fusion.43
  102.8 78.9 %all-gather.12.cloned.1.call-done = bf16[8192,2,2,128]{0,3,2,1:T(8,128)(2,1)} async-done(((bf16[256,2,2,128]{0,3,2,1:T(8,128)(2,1)}), bf16[8192,2,2,128]{0,3,2,1:T(8,128)(2,1)}) %all-gather.12.cloned.1.call-update) | async-done | bytes 8388624 | tf_op jit(solution)/shard_map/all_gather | solution.py:136
  181.7 9.5 %copy.75 = bf16[64,8,32,256]{3,2,1,0:T(8,128)(2,1)} copy(bf16[64,8,32,256]{3,1,2,0:T(8,128)(2,1)} %bitcast.106) | data formatting | bytes 16777216
  191.2 14.7 %copy.67 = bf16[32,256,2,2,128]{4,1,3,2,0:T(8,128)(2,1)} copy(bf16[32,256,2,2,128]{1,0,4,3,2:T(8,128)(2,1)} %bitcast.104) | data formatting | bytes 16777216
  205.9 40.4 %all-gather.10.cloned.1.call-done = bf16[32,256,2,128]{3,1,2,0:T(8,128)(2,1)} async-done(((bf16[1,256,2,128]{3,1,2,0:T(8,128)(2,1)}), bf16[32,256,2,128]{3,1,2,0:T(8,128)(2,1)}) %all-gather.10.cloned.1.call-update) | async-done | bytes 4194320 | tf_op jit(solution)/shard_map/all_gather | solution.py:138
  246.4 63.2 %all-gather.6.cloned.1.call-done = bf16[32,256,2,128]{3,1,2,0:T(8,128)(2,1)} async-done(((bf16[1,256,2,128]{3,1,2,0:T(8,128)(2,1)}), bf16[32,256,2,128]{3,1,2,0:T(8,128)(2,1)}) %all-gather.6.cloned.1.call-update) | async-done | bytes 4194320 | tf_op jit(solution)/shard_map/all_gather | solution.py:137
  310.1 352.1 %while.17 = (s32[]{:T(128)}, f32[256,2]{0,1:T(2,128)S(1)}, f32[256,2]{0,1:T(2,128)S(1)}, f32[256,2,128]{0,2,1:T(8,128)}, s32[32]{0:T(128)}, /*index=5*/s32[64]{0...) while((s32[]{:T(128)}, f32[256,2]{0,1:T(2,128)S(1)}, ...), condition=%wide.region_12.13_spmd.clone, body=%wide.region_6.12_spmd.clone.sunk | while | flops 137191712 | bytes 6097455 | solution.py:151
  321.0 1.3 dynamic_slice.59
  343.0 1.3 dynamic_slice.59
  387.0 1.3 dynamic_slice.59
  398.0 1.3 dynamic_slice.59
  431.0 1.3 dynamic_slice.59
  442.0 1.3 dynamic_slice.59
  486.1 1.3 dynamic_slice.59
  497.1 1.3 dynamic_slice.59
  541.1 1.3 dynamic_slice.59
  663.2 2.1 convolution_convert_fusion
  665.3 94.7 %reduce-scatter.2.cloned.1.call-done = bf16[32,4096]{1,0:T(8,128)(2,1)} async-done(((bf16[256,4096]{1,0:T(8,128)(2,1)}), bf16[32,4096]{1,0:T(8,128)(2,1)}) %reduce-scatter.2.cloned.1.call-update) | async-done | bytes 262160 | tf_op jit(solution)/shard_map/reduce_scatter | solution.py:157
  (655 shorter events, 305.4 us)
Async XLA Ops:
  6.5 656.6 %copy-start = (bf16[256,4096]{1,0:T(8,128)(2,1)S(1)}, bf16[256,4096]{1,0:T(8,128)(2,1)}, u32[]{:S(2)}) copy-start(bf16[256,4096]{1,0:T(8,128)(2,1)} %param.18) | copy-start | bytes 6291460
  6.5 81.9 %all-gather.8.cloned.1.call-start = ((), (), s32[]{:S(2)}) async-start(), calls=%async_computation.2 | async-start | bytes 2359296 | tf_op jit(solution)/shard_map/all_gather | solution.py:93
  7.3 174.4 %all-gather.12.cloned.1.call-start = ((), (), s32[]{:S(2)}) async-start(), calls=%async_computation.5 | async-start | bytes 8650752 | tf_op jit(solution)/shard_map/all_gather | solution.py:136
  14.5 6.5 copy-start.4
  14.5 6.5 copy-start.5
  88.4 4.4 copy-start.1
  92.8 3.9 copy-start.6
  96.7 2.3 copy-start.2
  96.7 3.2 copy-start.3
  98.9 147.4 %all-gather.10.cloned.1.call-start = ((), (), s32[]{:S(2)}) async-start(), calls=%async_computation.3 | async-start | bytes 4325376 | tf_op jit(solution)/shard_map/all_gather | solution.py:138
  99.9 209.6 %all-gather.6.cloned.1.call-start = ((), (), s32[]{:S(2)}) async-start(), calls=%async_computation.1 | async-start | bytes 4325376 | tf_op jit(solution)/shard_map/all_gather | solution.py:137
  100.8 659.2 %reduce-scatter.2.cloned.1.call-start = ((), (), s32[]{:S(2)}) async-start(), calls=%async_computation.4 | async-start | bytes 2359296 | tf_op jit(solution)/shard_map/reduce_scatter | solution.py:157
Sparse Core Ops, SparseCore 0:
  9.8 78.5 all-gather.7
  99.1 82.5 all-gather.11
  183.5 62.7 all-gather.9
  248.1 61.4 all-gather.5
  665.4 94.5 reduce-scatter.1
where the time goes:
time: 772 us; the launch traced here: 767 us
  waiting for transfers between devices  343 us (44%)
  matrix products  155 us (20%)
  local copies, waits for them, and re-layouts  113 us (15%)
  other arithmetic  95.6 us (12%)
  loops' own time  46.2 us (6%)
  between operations  13.3 us (2%)
    reduce_scatter x1, waiting for transfers between devices, body(): lax.psum_scatter(jnp.dot(heads_out, w_out, preferred_element_type=jnp.flo...  94.7 us
    all_gather x1, waiting for transfers between devices, body(): lax.all_gather(key_value[None], 'seq', axis=0, tiled=True)  78.9 us
    dot_general x64, matrix products, attend(): jnp.einsum('qhd,khd->qhk', queries, key_rows, preferred_element_type=jnp....  75.7 us
    dot_general x64, matrix products, attend(): jnp.einsum('qhk,khd->qhd', exp_terms.astype(jnp.bfloat16), values, prefer...  71.7 us
    all_gather x1, waiting for transfers between devices, body(): gathered = lax.all_gather(tokens, 'mp', axis=1, tiled=True)  65.4 us
    all_gather x1, waiting for transfers between devices, body(): lax.all_gather(prefix_keys, 'seq', axis=0, tiled=True)  63.2 us
    another operation x1, loops' own time, body(): lax.scan(scan_step, start_state, (sources, pieces[0], pieces[1], pieces[2]))  46.2 us
    dynamic_slice x32, local copies, waits for them, and re-layouts, body(): lax.scan(scan_step, start_state, (sources, pieces[0], pieces[1], pieces[2]))  41.8 us
  transfers between devices with their start and end apart: 5, of which 5 were waited for; matrix products, arithmetic and copies ran while one was open for 6% of the time, Pallas kernels for 0%

commit v1 on v0

v1 whole, which is shorter than its diff:
```python
import math

import jax
import jax.numpy as jnp
from jax import lax
from jax.sharding import PartitionSpec as P

HD = 128
PBLOCK = 128


NEG_FILL = -1e30


def layer_norm(rows_in, norm_gain, norm_bias):
    as_float = rows_in.astype(jnp.float32)
    row_mean = jnp.mean(as_float, -1, keepdims=True)
    centered = as_float - row_mean
    row_var = jnp.mean(centered * centered, -1, keepdims=True)
    scaled = centered * lax.rsqrt(row_var + 1e-05)
    return (scaled * norm_gain.astype(jnp.float32) + norm_bias.astype(jnp.float32)).astype(
        jnp.bfloat16
    )


def rotate(column_block, position):
    head_dim = column_block.shape[-1]
    half_rot = head_dim // 8
    inverse_freq = jnp.power(
        jnp.float32(10000.0), -jnp.arange(half_rot, dtype=jnp.float32) * (8.0 / head_dim)
    )
    angles = position.astype(jnp.float32)[:, None] * inverse_freq[None, :]
    cosine = jnp.cos(angles)[:, None, :]
    sines = jnp.sin(angles)[:, None, :]
    first_half = column_block[..., :half_rot]
    second = column_block[..., half_rot : 2 * half_rot]
    return jnp.concatenate(
        [
            first_half * cosine - second * sines,
            second * cosine + first_half * sines,
            column_block[..., 2 * half_rot :],
        ],
        -1,
    )


def request_info(global_index, lengths, context):
    request_end = jnp.cumsum(lengths)
    starts = request_end - lengths
    inside = (
        (global_index[:, None] >= starts[None, :]) & (global_index[:, None] < request_end[None, :])
    ).astype(jnp.int32)
    labels = jnp.arange(lengths.shape[0], dtype=jnp.int32) + 1
    request = jnp.sum(inside * labels[None, :], 1) - 1
    cached_len = jnp.sum(inside * context[None, :], 1)
    position = jnp.sum(inside * (context - starts)[None, :], 1) + global_index
    return (request, cached_len, position)


def masked_softmax_attention(queries, key_sets, value_sets, visible_sets):
    scale = 1.0 / math.sqrt(queries.shape[-1])
    score_sets = [
        jnp.einsum("qhd,khd->hqk", queries, keys, preferred_element_type=jnp.float32) * scale
        for keys in key_sets
    ]
    row_max = None
    for scores, visible in zip(score_sets, visible_sets):
        part = jnp.max(jnp.where(visible[None], scores, NEG_FILL), -1)
        row_max = part if row_max is None else jnp.maximum(row_max, part)
    row_sum = 0.0
    weighted = 0.0
    for scores, visible, values in zip(score_sets, visible_sets, value_sets):
        probs = jnp.where(visible[None], jnp.exp(scores - row_max[..., None]), 0.0)
        row_sum = row_sum + jnp.sum(probs, -1)
        weighted = weighted + jnp.einsum(
            "hqk,khd->hqd", probs.astype(jnp.bfloat16), values, preferred_element_type=jnp.float32
        )
    return weighted / row_sum[..., None]


SUFFIX_SHARDS = 5


def body(
    tokens,
    norm_gain,
    norm_bias,
    w_query,
    w_keyval,
    w_out,
    prefix_key,
    prefix_value,
    lengths,
    context,
    prefix_place,
):
    prefix_rows = prefix_key.shape[0]
    local_heads = w_query.shape[1] // HD
    prefix_both = lax.all_gather(
        jnp.stack([prefix_key, prefix_value], 0), "seq", axis=1, tiled=True
    )
    gathered = lax.all_gather(tokens, "mp", axis=1, tiled=True)
    token_count = gathered.shape[0]
    feature_count = gathered.shape[1]
    normed = layer_norm(gathered, norm_gain, norm_bias)
    seq_index = lax.axis_index("seq")
    seq_count = lax.psum(1, "seq")
    global_index = seq_index * token_count + jnp.arange(token_count, dtype=jnp.int32)
    request, cached_len, position = request_info(global_index, lengths, context)
    query_raw = jnp.dot(normed, w_query, preferred_element_type=jnp.float32).reshape(
        token_count, local_heads, HD
    )
    key_value_raw = jnp.dot(
        normed, w_keyval.reshape(feature_count, -1), preferred_element_type=jnp.float32
    ).reshape(token_count, 2, local_heads, HD)
    queries = rotate(query_raw, position).astype(jnp.bfloat16)
    own_keys = rotate(key_value_raw[:, 0], position).astype(jnp.bfloat16)
    own_values = key_value_raw[:, 1].astype(jnp.bfloat16)
    key_value = jnp.stack([own_keys, own_values], 0)

    window = [key_value]
    for shift in range(1, SUFFIX_SHARDS):
        pairs = [(i, i + shift) for i in range(seq_count - shift)]
        window.insert(0, lax.ppermute(key_value, "seq", pairs))
    window = jnp.concatenate(window, 1)
    window_count = window.shape[1]
    key_index = (seq_index - (SUFFIX_SHARDS - 1)) * token_count + jnp.arange(
        window_count, dtype=jnp.int32
    )
    key_request = request_info(key_index, lengths, context)[0]
    sees_suffix = (
        (key_index[None, :] >= 0)
        & (key_request[None, :] == request[:, None])
        & (key_index[None, :] <= global_index[:, None])
    )

    prefix_all = prefix_both.shape[1]
    prefix_position = (
        prefix_place[:, None] * PBLOCK + jnp.arange(PBLOCK, dtype=jnp.int32)[None, :]
    ).reshape(-1)
    sees_prefix = prefix_position[None, :] < cached_len[:, None]
    prefix_keys = prefix_both[0].reshape(prefix_all, local_heads, HD)
    prefix_values = prefix_both[1].reshape(prefix_all, local_heads, HD)

    attended = masked_softmax_attention(
        queries,
        (prefix_keys, window[0]),
        (prefix_values, window[1]),
        (sees_prefix, sees_suffix),
    )
    heads_out = (
        attended.astype(jnp.bfloat16).transpose(1, 0, 2).reshape(token_count, local_heads * HD)
    )
    summed = lax.psum_scatter(
        jnp.dot(heads_out, w_out, preferred_element_type=jnp.float32).astype(jnp.bfloat16),
        "mp",
        scatter_dimension=0,
        tiled=True,
    )
    return summed


def solution(mesh):
    return jax.shard_map(
        body,
        mesh=mesh,
        in_specs=(
            P("seq", "mp"),
            P(),
            P(),
            P(None, "mp"),
            P(None, None, "mp"),
            P("mp", None),
            P("seq", "mp"),
            P("seq", "mp"),
            P(),
            P(),
            P(),
        ),
        out_specs=P(("seq", "mp"), None),
        check_vma=False,
    )
```

time: 772 us -> 329 us (0.43)
  matrix products: 155 us -> 27.6 us
  waiting for transfers between devices: 343 us -> 230 us
  local copies, waits for them, and re-layouts: 113 us -> 28.3 us
  other arithmetic: 95.6 us -> 17 us
  loops' own time: 46.2 us -> 0 us
  starting transfers between devices: 0.17 us -> 12.7 us
    all_gather x3 -> x1, waiting for transfers between devices: 182 us -> 45.9 us  [body(): lax.all_gather(jnp.stack([prefix_key, prefix_value], 0), 'seq', axis=1, t...]
    dot_general x128 -> x4, matrix products: 147 us -> 19.9 us  [the longest x2 10.2 us: masked_softmax_attention(): jnp.einsum('hqk,khd->hqd', probs.astype(jnp.bfloat16), values, preferred_...]
    another operation x1 -> x0, loops' own time: 46.2 us -> none  [body(): lax.scan(scan_step, start_state, (sources, pieces[0], pieces[1], pieces[2]))]
    dynamic_slice x32 -> x0, local copies, waits for them, and re-layouts: 41.8 us -> none  [body(): lax.scan(scan_step, start_state, (sources, pieces[0], pieces[1], pieces[2]))]
    squeeze x32 -> x0, local copies, waits for them, and re-layouts: 31.2 us -> none  [body(): lax.scan(scan_step, start_state, (sources, pieces[0], pieces[1], pieces[2]))]
    reduce_sum x33 -> x2, other arithmetic: 26 us -> 0.19 us  [request_info(): request = jnp.sum(inside * labels[None, :], 1) - 1]
    ppermute x0 -> x4, waiting for transfers between devices: none -> 25.1 us  [body(): window.insert(0, lax.ppermute(key_value, 'seq', pairs))]
    and x32 -> x1, other arithmetic: 25.3 us -> 0.41 us  [body(): (key_index[None, :] >= 0) & (key_request[None, :] == request[:, None])]
  transfers between devices with their start and end apart: 5 -> 7, of which waited for: 5 -> 5; matrix products, arithmetic and copies ran while one was open for 6% -> 12% of each run, Pallas kernels for 0% -> 0%
where the time goes in v1:
time: 329 us
  waiting for transfers between devices  230 us (70%)
  local copies, waits for them, and re-layouts  28.3 us (9%)
  matrix products  27.6 us (8%)
  other arithmetic  17 us (5%)
  between operations  13.5 us (4%)
  starting transfers between devices  12.7 us (4%)
    reduce_scatter x1, waiting for transfers between devices, body(): lax.psum_scatter(jnp.dot(heads_out, w_out, preferred_element_type=jnp.flo...  96.6 us
    all_gather x1, waiting for transfers between devices, body(): gathered = lax.all_gather(tokens, 'mp', axis=1, tiled=True)  61.3 us
    all_gather x1, waiting for transfers between devices, body(): lax.all_gather(jnp.stack([prefix_key, prefix_value], 0), 'seq', axis=1, t...  45.9 us
    ppermute x4, waiting for transfers between devices, body(): window.insert(0, lax.ppermute(key_value, 'seq', pairs))  25.1 us
    unnamed x40, local copies, waits for them, and re-layouts  13.8 us
    ppermute x4, starting transfers between devices, body(): window.insert(0, lax.ppermute(key_value, 'seq', pairs))  12.6 us
    dot_general x2, matrix products, masked_softmax_attention(): jnp.einsum('hqk,khd->hqd', probs.astype(jnp.bfloat16), values, preferred_...  10.2 us
    dot_general x2, matrix products, masked_softmax_attention(): jnp.einsum('qhd,khd->hqk', queries, keys, preferred_element_type=jnp.floa...  9.72 us
  transfers between devices with their start and end apart: 7, of which 5 were waited for; matrix products, arithmetic and copies ran while one was open for 12% of the time, Pallas kernels for 0%

profile of v1, /device:TPU:2, one launch (start us, length us, event | category | flops | bytes accessed | tf_op | source)
XLA Modules:
  0.0 328.7 jit_solution(272534547121617955)
XLA Ops:
  12.4 4.9 %copy.63 = bf16[512,8,2,256]{3,1,2,0:T(8,128)(2,1)} copy(bf16[512,8,2,256]{3,2,1,0:T(2,128)(2,1)} %bitcast.52) | data formatting | bytes 8388608
  17.3 6.4 %copy.52 = bf16[512,4096]{1,0:T(8,128)(2,1)} copy(bf16[512,4096]{0,1:T(8,128)(2,1)} %bitcast.51) | data formatting | bytes 8388608 | tf_op jit(solution)/shard_map/dot_general | solution.py:113
  24.5 2.6 broadcast_compare_fusion
  27.1 61.3 %all-gather.3.cloned.1.call-done = bf16[256,4096]{1,0:T(8,128)(2,1)} async-done(((bf16[256,512]{1,0:T(8,128)(2,1)}), bf16[256,4096]{1,0:T(8,128)(2,1)}) %all-gather.3.cloned.1.call-update) | async-done | bytes 2097168 | tf_op jit(solution)/shard_map/all_gather | solution.py:102
  88.4 2.1 convert_reduce_fusion
  90.5 2.3 fusion.7
  92.8 1.4 fusion.41
  94.5 4.1 %fusion.13 = f32[256,2,2,128]{3,0,2,1:T(8,128)S(1)} fusion(bf16[2,2,128,4096]{3,2,1,0:T(8,128)(2,1)} %bitcast.53, bf16[256,4096]{1,0:T(8,128)(2,1)} %all-gather.3.cloned.1.call-done, f32[4096]{0:T(1024)S(1)} %convert_element_type.57, f32[4096]{0:T(1024)S(1)} %convert_element_type.56, f32[256]{0:T(256)S(1)} %add_rsqrt_fusion, f32[256]{0:T(256)S(1)} %broadcast_multiply_fusion), kind=kOutput, calls=%fused_computation.21 | convolution fusion | flops 1080033280 | bytes 6850560 | tf_op jit(solution)/shard_map/dot_general | solution.py:113
  99.9 2.8 collective-permute-start
  102.7 1.9 collective-permute-start.1
  104.6 3.6 %collective-permute-start.2 = (bf16[2,256,2,128]{3,1,2,0:T(8,128)(2,1)S(1)}, bf16[2,256,2,128]{3,1,2,0:T(8,128)(2,1)}, u32[]{:S(2)}, u32[]{:S(2)}) collective-permute-start(bf16[2,256,2,128]{3,1,2,0:T(8,128)(2,1)S(1)} %pad_maximum_fusion.1), channel_id=1, source_target_pairs={{0,16},{8,24},{16,32},{24,40},{32,48},{40,56},{48,64},{56,72},{64,... | collective-permute-start | bytes 786440 | tf_op jit(solution)/shard_map/ppermute | solution.py:124
  109.6 4.3 %collective-permute-start.3 = (bf16[2,256,2,128]{3,1,2,0:T(8,128)(2,1)S(1)}, bf16[2,256,2,128]{3,1,2,0:T(8,128)(2,1)}, u32[]{:S(2)}, u32[]{:S(2)}) collective-permute-start(bf16[2,256,2,128]{3,1,2,0:T(8,128)(2,1)S(1)} %pad_maximum_fusion.1), channel_id=1, source_target_pairs={{0,8},{8,16},{16,24},{24,32},{32,40},{40,48},{48,56},{56,64},{64,7... | collective-permute-start | bytes 786440 | tf_op jit(solution)/shard_map/ppermute | solution.py:124
  114.6 22.2 %collective-permute-done = bf16[2,256,2,128]{3,1,2,0:T(8,128)(2,1)} collective-permute-done((bf16[2,256,2,128]{3,1,2,0:T(8,128)(2,1)S(1)}, bf16[2,256,2,128]{3,1,2,0:T(8,128)(2,1)}, u32[]{:S(2)}, u32[]{:S(2)}) %collective-permute-start) | collective-permute-done | bytes 262176 | tf_op jit(solution)/shard_map/ppermute | solution.py:124
  137.8 2.9 collective-permute-done.1
  142.7 1.0 constant_dynamic-update-slice_fusion.1
  143.9 1.0 copy-done.9
  145.0 3.3 select_reduce_fusion.1
  148.3 45.9 %all-gather.5.cloned.1.call-done = bf16[2,8192,256]{1,2,0:T(8,128)(2,1)} async-done(((bf16[2,256,256]{1,2,0:T(8,128)(2,1)}), bf16[2,8192,256]{1,2,0:T(8,128)(2,1)}) %all-gather.5.cloned.1.call-update) | async-done | bytes 8388624 | tf_op jit(solution)/shard_map/all_gather | solution.py:99
  194.1 6.0 %fusion.44 = (bf16[1,8192,256]{1,2,0:T(8,128)(2,1)}, bf16[1,8192,256]{1,2,0:T(8,128)(2,1)}) fusion(bf16[2,8192,256]{1,2,0:T(8,128)(2,1)} %all-gather.5.cloned.1.call-done), kind=kLoop, calls=%fused_computation.79 | loop fusion | bytes 16777216 | tf_op jit(solution)/shard_map/slice | solution.py:142
  200.2 6.4 %select_reduce_fusion = (f32[2,256]{1,0:T(2,128)S(1)}, f32[2,256,8192]{2,1,0:T(8,128)S(1)}) fusion(pred[256,8192]{1,0:T(8,128)(4,1)S(1)} %copy-done.2, bf16[8192,2,128]{0,2,1:T(8,128)(2,1)} %bitcast.55, bf16[256,2,96]{2,0,1:T(8,128)(2,1)S(1)} %copy-done.7, bf16[256,2,16]{2,0,1:T(8,128)(2,1)S(1)} %copy-done.5, bf16[256,2,16]{2,0,1:T(8,128)(2,1)S(1)} %copy-done.6), kind=kOutput, calls=%fused_computation.1 | convolution fusion | flops 1086717440 | bytes 23201792 | tf_op jit(solution)/shard_map/qhd,khd->hqk/dot_general | solution.py:63
  206.7 4.8 %fusion = f32[2,256]{1,0:T(2,128)S(1)} fusion(f32[2,256,8192]{2,1,0:T(8,128)S(1)} %get-tuple-element.23, f32[2,256]{1,0:T(2,128)S(1)} %max.7, pred[256,8192]{1,0:T(8,128)(4,1)S(1)} %copy-done.2), kind=kLoop, calls=%fused_computation.2 | loop fusion | flops 16776704 | bytes 18878464 | tf_op jit(solution)/shard_map/reduce_sum | solution.py:74
  212.4 9.4 %fusion.2 = f32[2,256,128]{1,2,0:T(8,128)S(1)} fusion(bf16[8192,2,128]{0,2,1:T(8,128)(2,1)} %bitcast.54, f32[2,256,8192]{2,1,0:T(8,128)} %copy-done.1, f32[2,256]{1,0:T(2,128)S(1)} %max.7, pred[256,8192]{1,0:T(8,128)(4,1)S(1)} %copy-done.2), kind=kOutput, calls=%fused_computation.4 | convolution fusion | flops 1090519040 | bytes 23332864 | tf_op jit(solution)/shard_map/hqk,khd->hqd/dot_general | solution.py:75
  223.4 2.1 convolution_convert_fusion
  225.5 96.6 %reduce-scatter.2.cloned.1.call-done = bf16[32,4096]{1,0:T(8,128)(2,1)} async-done(((bf16[256,4096]{1,0:T(8,128)(2,1)}), bf16[32,4096]{1,0:T(8,128)(2,1)}) %reduce-scatter.2.cloned.1.call-update) | async-done | bytes 262160 | tf_op jit(solution)/shard_map/reduce_scatter | solution.py:154
  (81 shorter events, 15.7 us)
Async XLA Ops:
  6.5 216.9 %copy-start = (bf16[256,4096]{1,0:T(8,128)(2,1)S(1)}, bf16[256,4096]{1,0:T(8,128)(2,1)}, u32[]{:S(2)}) copy-start(bf16[256,4096]{1,0:T(8,128)(2,1)} %param.16) | copy-start | bytes 6291460
  6.5 81.9 %all-gather.3.cloned.1.call-start = ((), (), s32[]{:S(2)}) async-start(), calls=%async_computation.1 | async-start | bytes 2359296 | tf_op jit(solution)/shard_map/all_gather | solution.py:102
  7.3 186.9 %all-gather.5.cloned.1.call-start = ((), (), s32[]{:S(2)}) async-start(), calls=%async_computation.2 | async-start | bytes 8650752 | tf_op jit(solution)/shard_map/all_gather | solution.py:99
  10.1 312.1 %reduce-scatter.2.cloned.1.call-start = ((), (), s32[]{:S(2)}) async-start(), calls=%async_computation.3 | async-start | bytes 2359296 | tf_op jit(solution)/shard_map/reduce_scatter | solution.py:154
  17.3 6.5 %copy-start.11 = (s32[16]{0:T(128)S(1)}, s32[16]{0:T(128)}, u32[]{:S(2)}) copy-start(s32[16]{0:T(128)} %param.19) | copy-start | bytes 196
  17.3 6.5 %copy-start.12 = (s32[16]{0:T(128)S(1)}, s32[16]{0:T(128)}, u32[]{:S(2)}) copy-start(s32[16]{0:T(128)} %param.20) | copy-start | bytes 196
  17.3 7.1 %copy-start.14 = (s32[64]{0:T(128)S(1)}, s32[64]{0:T(128)}, u32[]{:S(2)}) copy-start(s32[64]{0:T(128)} %param.21) | copy-start | bytes 772
  88.4 4.4 %copy-start.3 = (bf16[256,4096]{1,0:T(8,128)(2,1)S(1)}, bf16[256,4096]{1,0:T(8,128)(2,1)}, u32[]{:S(2)}) copy-start(bf16[256,4096]{1,0:T(8,128)(2,1)} %all-gather.3.cloned.1.call-done) | copy-start | bytes 6291460
  88.4 4.4 %copy-start.13 = (bf16[4096,256]{1,0:T(8,128)(2,1)S(1)}, bf16[4096,256]{1,0:T(8,128)(2,1)}, u32[]{:S(2)}) copy-start(bf16[4096,256]{1,0:T(8,128)(2,1)} %param.14) | copy-start | bytes 6291460
  94.3 4.4 %copy-start.8 = (f32[256,256]{0,1:T(8,128)}, f32[256,256]{0,1:T(8,128)S(1)}, u32[]{:S(2)}) copy-start(f32[256,256]{0,1:T(8,128)S(1)} %fusion.41) | copy-start | bytes 786436
  99.7 45.2 %copy-start.5 = (bf16[256,2,16]{2,0,1:T(8,128)(2,1)S(1)}, bf16[256,2,16]{2,0,1:T(8,128)(2,1)}, u32[]{:S(2)}) copy-start(bf16[256,2,16]{2,0,1:T(8,128)(2,1)} %get-tuple-element.16) | copy-start | bytes 49156
  99.9 36.9 %collective-permute-start = (bf16[2,256,2,128]{3,1,2,0:T(8,128)(2,1)S(1)}, bf16[2,256,2,128]{3,1,2,0:T(8,128)(2,1)}, u32[]{:S(2)}, u32[]{:S(2)}) collective-permute-start(bf16[2,256,2,128]{3,1,2,0:T(8,128)(2,1)S(1)} %pad_maximum_fusion.1), channel_id=1, source_target_pairs={{0,32},{8,40},{16,48},{24,56},{32,64},{40,72},{48,80},{56,88},{64,... | collective-permute-start | bytes 786440 | tf_op jit(solution)/shard_map/ppermute | solution.py:124
  102.7 38.0 %collective-permute-start.1 = (bf16[2,256,2,128]{3,1,2,0:T(8,128)(2,1)S(1)}, bf16[2,256,2,128]{3,1,2,0:T(8,128)(2,1)}, u32[]{:S(2)}, u32[]{:S(2)}) collective-permute-start(bf16[2,256,2,128]{3,1,2,0:T(8,128)(2,1)S(1)} %pad_maximum_fusion.1), channel_id=1, source_target_pairs={{0,24},{8,32},{16,40},{24,48},{32,56},{40,64},{48,72},{56,80},{64,... | collective-permute-start | bytes 786440 | tf_op jit(solution)/shard_map/ppermute | solution.py:124
  104.6 37.1 %collective-permute-start.2 = (bf16[2,256,2,128]{3,1,2,0:T(8,128)(2,1)S(1)}, bf16[2,256,2,128]{3,1,2,0:T(8,128)(2,1)}, u32[]{:S(2)}, u32[]{:S(2)}) collective-permute-start(bf16[2,256,2,128]{3,1,2,0:T(8,128)(2,1)S(1)} %pad_maximum_fusion.1), channel_id=1, source_target_pairs={{0,16},{8,24},{16,32},{24,40},{32,48},{40,56},{48,64},{56,72},{64,... | collective-permute-start | bytes 786440 | tf_op jit(solution)/shard_map/ppermute | solution.py:124
  109.6 33.1 %collective-permute-start.3 = (bf16[2,256,2,128]{3,1,2,0:T(8,128)(2,1)S(1)}, bf16[2,256,2,128]{3,1,2,0:T(8,128)(2,1)}, u32[]{:S(2)}, u32[]{:S(2)}) collective-permute-start(bf16[2,256,2,128]{3,1,2,0:T(8,128)(2,1)S(1)} %pad_maximum_fusion.1), channel_id=1, source_target_pairs={{0,8},{8,16},{16,24},{24,32},{32,40},{40,48},{48,56},{56,64},{64,7... | collective-permute-start | bytes 786440 | tf_op jit(solution)/shard_map/ppermute | solution.py:124
  143.9 1.1 copy-start.9
  148.3 51.9 %copy-start.6 = (bf16[256,2,16]{2,0,1:T(8,128)(2,1)S(1)}, bf16[256,2,16]{2,0,1:T(8,128)(2,1)}, u32[]{:S(2)}) copy-start(bf16[256,2,16]{2,0,1:T(8,128)(2,1)} %get-tuple-element.17) | copy-start | bytes 49156
  148.3 51.9 %copy-start.7 = (bf16[256,2,96]{2,0,1:T(8,128)(2,1)S(1)}, bf16[256,2,96]{2,0,1:T(8,128)(2,1)}, u32[]{:S(2)}) copy-start(bf16[256,2,96]{2,0,1:T(8,128)(2,1)} %copy.62) | copy-start | bytes 294916
  194.1 6.0 %copy-start.2 = (pred[256,8192]{1,0:T(8,128)(4,1)S(1)}, pred[256,8192]{1,0:T(8,128)(4,1)}, u32[]{:S(2)}) copy-start(pred[256,8192]{1,0:T(8,128)(4,1)} %broadcast_compare_fusion) | copy-start | bytes 6291460
  206.6 5.7 %copy-start.1 = (f32[2,256,8192]{2,1,0:T(8,128)}, f32[2,256,8192]{2,1,0:T(8,128)S(1)}, u32[]{:S(2)}) copy-start(f32[2,256,8192]{2,1,0:T(8,128)S(1)} %get-tuple-element.23) | copy-start | bytes 50331652
  212.3 9.5 %copy-start.4 = (f32[2,256,1280]{2,1,0:T(8,128)S(1)}, f32[2,256,1280]{2,1,0:T(8,128)}, u32[]{:S(2)}) copy-start(f32[2,256,1280]{2,1,0:T(8,128)} %get-tuple-element.25) | copy-start | bytes 7864324
  212.3 10.3 %copy-start.10 = (bf16[2,1280,2,128]{3,1,2,0:T(8,128)(2,1)S(1)}, bf16[2,1280,2,128]{3,1,2,0:T(8,128)(2,1)}, u32[]{:S(2)}) copy-start(bf16[2,1280,2,128]{3,1,2,0:T(8,128)(2,1)} %copy-done.9) | copy-start | bytes 3932164
Sparse Core Ops, SparseCore 0:
  9.8 78.5 all-gather.2
  90.2 103.9 all-gather.4
  225.7 96.4 reduce-scatter.1

commit v2 on v1

--- a/solution.py
+++ b/solution.py
@@ -81,6 +81,27 @@
 SUFFIX_SHARDS = 5
 
 
+def gather_features(tokens):
+    mp_count = lax.psum(1, "mp")
+    ring = mp_count // 2
+    mp_index = lax.axis_index("mp")
+    partner = lax.ppermute(tokens, "mp", [(i, i ^ 1) for i in range(mp_count)])
+    pair = jnp.where(
+        mp_index % 2 == 0,
+        jnp.concatenate([tokens, partner], 1),
+        jnp.concatenate([partner, tokens], 1),
+    )
+    blocks = [pair]
+    for shift in range(1, ring):
+        blocks.append(
+            lax.ppermute(pair, "mp", [(i, (i + 2 * shift) % mp_count) for i in range(mp_count)])
+        )
+    ring_index = mp_index // 2
+    order = (ring_index - jnp.arange(ring, dtype=jnp.int32)) % ring
+    stacked = jnp.stack(blocks, 0)[order]
+    return stacked.transpose(1, 0, 2).reshape(tokens.shape[0], -1)
+
+
 def body(
     tokens,
     norm_gain,
@@ -99,7 +120,7 @@
     prefix_both = lax.all_gather(
         jnp.stack([prefix_key, prefix_value], 0), "seq", axis=1, tiled=True
     )
-    gathered = lax.all_gather(tokens, "mp", axis=1, tiled=True)
+    gathered = gather_features(tokens)
     token_count = gathered.shape[0]
     feature_count = gathered.shape[1]
     normed = layer_norm(gathered, norm_gain, norm_bias)
@@ -151,13 +172,12 @@
     heads_out = (
         attended.astype(jnp.bfloat16).transpose(1, 0, 2).reshape(token_count, local_heads * HD)
     )
-    summed = lax.psum_scatter(
-        jnp.dot(heads_out, w_out, preferred_element_type=jnp.float32).astype(jnp.bfloat16),
-        "mp",
-        scatter_dimension=0,
-        tiled=True,
-    )
-    return summed
+    partial = jnp.dot(heads_out, w_out, preferred_element_type=jnp.float32).astype(jnp.bfloat16)
+    mp_count = lax.psum(1, "mp")
+    exchanged = lax.all_to_all(
+        partial.reshape(mp_count, token_count // mp_count, -1), "mp", 0, 0, tiled=False
+    )
+    return jnp.sum(exchanged.astype(jnp.float32), 0).astype(jnp.bfloat16)
 
 
 def solution(mesh):

time: 329 us -> 227 us (0.69); the launches traced: 329 us -> 223 us
  waiting for transfers between devices: 230 us -> 48.3 us
  blocking collectives: 0 us -> 55.9 us
  starting transfers between devices: 12.7 us -> 24.3 us
  local copies, waits for them, and re-layouts: 28.3 us -> 34.8 us
  other arithmetic: 17 us -> 21.8 us
  matrix products: 27.6 us -> 24.3 us
    reduce_scatter x1 -> x0, waiting for transfers between devices: 96.6 us -> none  [body(): lax.psum_scatter(jnp.dot(heads_out, w_out, preferred_element_type=jnp.flo...]
    all_gather x1 -> x0, waiting for transfers between devices: 61.3 us -> none  [body(): gathered = lax.all_gather(tokens, 'mp', axis=1, tiled=True)]
    all_to_all x0 -> x1, blocking collectives: none -> 55.9 us  [body(): lax.all_to_all(partial.reshape(mp_count, token_count // mp_count, -1), 'm...]
    all_gather x1, waiting for transfers between devices: 45.9 us -> 0.01 us  [body(): lax.all_gather(jnp.stack([prefix_key, prefix_value], 0), 'seq', axis=1, t...]
    ppermute x0 -> x4, waiting for transfers between devices: none -> 24 us  [the longest x3 24 us: gather_features(): lax.ppermute(pair, 'mp', [(i, (i + 2 * shift) % mp_count) for i in range(...]
    ppermute x0 -> x4, starting transfers between devices: none -> 12 us  [the longest x1 7.28 us: gather_features(): partner = lax.ppermute(tokens, 'mp', [(i, i ^ 1) for i in range(mp_count)])]
    dot_general x0 -> x1, local copies, waits for them, and re-layouts: none -> 4.15 us  [body(): jnp.dot(normed, w_query, preferred_element_type=jnp.float32)]
    unnamed x40 -> x31, local copies, waits for them, and re-layouts: 13.8 us -> 9.83 us
  transfers between devices with their start and end apart: 7 -> 9, of which waited for: 5 -> 4; matrix products, arithmetic and copies ran while one was open for 12% -> 20% of each run, Pallas kernels for 0% -> 0%
where the time goes in v2:
time: 227 us; the launch traced here: 223 us
  blocking collectives  55.9 us (25%)
  waiting for transfers between devices  48.3 us (21%)
  local copies, waits for them, and re-layouts  34.8 us (15%)
  starting transfers between devices  24.3 us (11%)
  matrix products  24.3 us (11%)
  other arithmetic  21.8 us (10%)
  between operations  13.8 us (6%)
    all_to_all x1, blocking collectives, body(): lax.all_to_all(partial.reshape(mp_count, token_count // mp_count, -1), 'm...  55.9 us
    ppermute x4, waiting for transfers between devices, body(): window.insert(0, lax.ppermute(key_value, 'seq', pairs))  24.3 us
    ppermute x3, waiting for transfers between devices, gather_features(): lax.ppermute(pair, 'mp', [(i, (i + 2 * shift) % mp_count) for i in range(...  24 us
    ppermute x4, starting transfers between devices, body(): window.insert(0, lax.ppermute(key_value, 'seq', pairs))  12.3 us
    dot_general x2, matrix products, masked_softmax_attention(): jnp.einsum('hqk,khd->hqd', probs.astype(jnp.bfloat16), values, preferred_...  10.1 us
    unnamed x31, local copies, waits for them, and re-layouts  9.83 us
    dot_general x2, matrix products, masked_softmax_attention(): jnp.einsum('qhd,khd->hqk', queries, keys, preferred_element_type=jnp.floa...  8.36 us
    ppermute x1, starting transfers between devices, gather_features(): partner = lax.ppermute(tokens, 'mp', [(i, i ^ 1) for i in range(mp_count)])  7.28 us
  transfers between devices with their start and end apart: 9, of which 4 were waited for; matrix products, arithmetic and copies ran while one was open for 20% of the time, Pallas kernels for 0%

profile of v2, /device:TPU:2, one launch (start us, length us, event | category | flops | bytes accessed | tf_op | source)
XLA Modules:
  0.0 223.2 jit_solution(14693601259821718476)
XLA Ops:
  9.5 7.3 %collective-permute-start = (bf16[256,512]{1,0:T(8,128)(2,1)}, bf16[256,512]{1,0:T(8,128)(2,1)S(1)}, u32[]{:S(2)}, u32[]{:S(2)}) collective-permute-start(bf16[256,512]{1,0:T(8,128)(2,1)} %param.11), channel_id=1, source_target_pairs={{0,1},{1,0},{2,3},{3,2},{4,5},{5,4},{6,7},{7,6},{8,9},{9,8},{10,11... | collective-permute-start | bytes 786440 | tf_op jit(solution)/shard_map/ppermute | solution.py:88
  20.0 2.6 %broadcast_compare_fusion = pred[256,8192]{1,0:T(8,128)(4,1)} fusion(s32[8192]{0:T(1024)S(1)} %add_bitcast_fusion, s32[256]{0:T(256)S(1)} %get-tuple-element.7), kind=kLoop, calls=%fused_computation.16 | loop fusion | flops 2097152 | bytes 2130944 | tf_op jit(solution)/shard_map/lt | solution.py:162
  22.7 4.1 %copy.61 = bf16[256,4096]{1,0:T(8,128)(2,1)} copy(bf16[256,4096]{0,1:T(8,128)(2,1)} %bitcast.73) | data formatting | bytes 4194304 | tf_op jit(solution)/shard_map/dot_general | solution.py:131
  26.8 4.9 %copy.63 = bf16[512,8,2,256]{3,1,2,0:T(8,128)(2,1)} copy(bf16[512,8,2,256]{3,2,1,0:T(2,128)(2,1)} %bitcast.69) | data formatting | bytes 8388608
  31.7 6.4 %copy.50 = bf16[512,4096]{1,0:T(8,128)(2,1)} copy(bf16[512,4096]{0,1:T(8,128)(2,1)} %bitcast.64) | data formatting | bytes 8388608 | tf_op jit(solution)/shard_map/dot_general | solution.py:134
  38.3 3.1 %collective-permute-start.3 = (bf16[256,1024]{1,0:T(8,128)(2,1)S(1)}, bf16[256,1024]{1,0:T(8,128)(2,1)S(1)}, u32[]{:S(2)}, u32[]{:S(2)}) collective-permute-start(bf16[256,1024]{1,0:T(8,128)(2,1)S(1)} %maximum_select_fusion.1), channel_id=1, source_target_pairs={{0,6},{1,7},{2,0},{3,1},{4,2},{5,3},{6,4},{7,5},{8,14},{9,15},{10,... | collective-permute-start | bytes 1572872 | tf_op jit(solution)/shard_map/ppermute | solution.py:97
  43.3 20.3 %collective-permute-done.3 = bf16[256,1024]{1,0:T(8,128)(2,1)S(1)} collective-permute-done((bf16[256,1024]{1,0:T(8,128)(2,1)S(1)}, bf16[256,1024]{1,0:T(8,128)(2,1)S(1)}, u32[]{:S(2)}, u32[]{:S(2)}) %collective-permute-start.3) | collective-permute-done | bytes 524320 | tf_op jit(solution)/shard_map/ppermute | solution.py:97
  63.5 3.7 %collective-permute-done.1 = bf16[256,1024]{1,0:T(8,128)(2,1)S(1)} collective-permute-done((bf16[256,1024]{1,0:T(8,128)(2,1)S(1)}, bf16[256,1024]{1,0:T(8,128)(2,1)S(1)}, u32[]{:S(2)}, u32[]{:S(2)}) %collective-permute-start.1) | collective-permute-done | bytes 524320 | tf_op jit(solution)/shard_map/ppermute | solution.py:97
  68.9 3.6 %gather_fusion = bf16[4,256,1024]{2,1,0:T(8,128)(2,1)} fusion(bf16[4,256,1024]{2,1,0:T(8,128)(2,1)} %pad_maximum_fusion, s32[1024]{0:T(1024)S(1)} %pad_clamp_fusion), kind=kCustom, calls=%fused_computation | custom fusion | bytes 4194320 | tf_op jit(solution)/shard_map/gather | solution.py:101
  75.6 2.4 %fusion.13 = bf16[256,4,1024]{2,0,1:T(8,128)(2,1)} fusion(bf16[4,256,1024]{2,1,0:T(8,128)(2,1)S(1)} %copy-done.1, f32[4,1024]{1,0:T(4,128)S(1)} %reshape.474, f32[4,1024]{1,0:T(4,128)S(1)} %reshape.473, f32[256]{0:T(256)S(1)} %add_rsqrt_fusion, f32[256]{0:T(256)S(1)} %broadcast_multiply_fusion), kind=kLoop, calls=%fused_computation.22 | loop fusion | flops 6291456 | bytes 4229120 | tf_op jit(solution)/shard_map/convert_element_type | solution.py:21
  77.9 4.0 %copy.43 = bf16[256,4,1024]{0,2,1:T(8,128)(2,1)} copy(bf16[256,4,1024]{2,0,1:T(8,128)(2,1)} %fusion.13) | data formatting | bytes 4194304 | tf_op jit(solution)/shard_map/convert_element_type | solution.py:21
  81.9 4.4 %fusion.46 = f32[256,2,2,128]{0,3,2,1:T(8,128)S(1)} fusion(bf16[256,4096,1,1]{0,1,3,2:T(8,128)(2,1)} %bitcast.66, bf16[2,2,128,4096]{3,2,1,0:T(8,128)(2,1)} %bitcast.70), kind=kOutput, calls=%fused_computation.93 | convolution fusion | flops 1073741824 | bytes 6815744 | tf_op jit(solution)/shard_map/dot_general | solution.py:134
  87.1 3.4 %collective-permute-start.4 = (bf16[2,256,2,128]{1,3,2,0:T(8,128)(2,1)S(1)}, bf16[2,256,2,128]{1,3,2,0:T(8,128)(2,1)S(1)}, u32[]{:S(2)}, u32[]{:S(2)}) collective-permute-start(bf16[2,256,2,128]{1,3,2,0:T(8,128)(2,1)S(1)} %pad_maximum_fusion.2), channel_id=1, source_target_pairs={{0,32},{8,40},{16,48},{24,56},{32,64},{40,72},{48,80},{56,88},{64,... | collective-permute-start | bytes 786440 | tf_op jit(solution)/shard_map/ppermute | solution.py:145
  92.8 3.7 %collective-permute-start.6 = (bf16[2,256,2,128]{1,3,2,0:T(8,128)(2,1)S(1)}, bf16[2,256,2,128]{1,3,2,0:T(8,128)(2,1)S(1)}, u32[]{:S(2)}, u32[]{:S(2)}) collective-permute-start(bf16[2,256,2,128]{1,3,2,0:T(8,128)(2,1)S(1)} %pad_maximum_fusion.2), channel_id=1, source_target_pairs={{0,16},{8,24},{16,32},{24,40},{32,48},{40,56},{48,64},{56,72},{64,... | collective-permute-start | bytes 786440 | tf_op jit(solution)/shard_map/ppermute | solution.py:145
  97.0 3.0 %collective-permute-start.7 = (bf16[2,256,2,128]{1,3,2,0:T(8,128)(2,1)S(1)}, bf16[2,256,2,128]{1,3,2,0:T(8,128)(2,1)S(1)}, u32[]{:S(2)}, u32[]{:S(2)}) collective-permute-start(bf16[2,256,2,128]{1,3,2,0:T(8,128)(2,1)S(1)} %pad_maximum_fusion.2), channel_id=1, source_target_pairs={{0,8},{8,16},{16,24},{24,32},{32,40},{40,48},{48,56},{56,64},{64,7... | collective-permute-start | bytes 786440 | tf_op jit(solution)/shard_map/ppermute | solution.py:145
  99.9 21.9 %collective-permute-done.4 = bf16[2,256,2,128]{1,3,2,0:T(8,128)(2,1)S(1)} collective-permute-done((bf16[2,256,2,128]{1,3,2,0:T(8,128)(2,1)S(1)}, bf16[2,256,2,128]{1,3,2,0:T(8,128)(2,1)S(1)}, u32[]{:S(2)}, u32[]{:S(2)}) %collective-permute-start.4) | collective-permute-done | bytes 262176 | tf_op jit(solution)/shard_map/ppermute | solution.py:145
  121.9 2.4 %collective-permute-done.5 = bf16[2,256,2,128]{1,3,2,0:T(8,128)(2,1)S(1)} collective-permute-done((bf16[2,256,2,128]{1,3,2,0:T(8,128)(2,1)S(1)}, bf16[2,256,2,128]{1,3,2,0:T(8,128)(2,1)S(1)}, u32[]{:S(2)}, u32[]{:S(2)}) %collective-permute-start.5) | collective-permute-done | bytes 262176 | tf_op jit(solution)/shard_map/ppermute | solution.py:145
  125.5 2.3 %select_reduce_fusion.1 = (f32[2,256]{1,0:T(2,128)S(1)}, f32[2,256,1280]{2,1,0:T(8,128)}) fusion(pred[256,1280]{1,0:T(8,128)(4,1)S(1)} %compare_and_fusion, bf16[2,1280,2,128]{1,3,2,0:T(8,128)(2,1)S(1)} %constant_dynamic-update-slice_fusion, bf16[256,2,96]{0,2,1:T(8,128)(2,1)S(1)} %slice.93, bf16[256,2,16]{0,2,1:T(8,128)(2,1)S(1)} %get-tuple-element.16, ...), kind=kOutput, calls=%fused_computation.19 | convolution fusion | flops 170130944 | bytes 3737600 | tf_op jit(solution)/shard_map/qhd,khd->hqk/dot_general | solution.py:63
  127.8 6.0 %fusion.44 = (bf16[1,8192,256]{1,2,0:T(8,128)(2,1)}, bf16[1,8192,256]{1,2,0:T(8,128)(2,1)}) fusion(bf16[2,8192,256]{1,2,0:T(8,128)(2,1)} %all-gather.2.cloned.1.call-done), kind=kLoop, calls=%fused_computation.91 | loop fusion | bytes 16777216 | tf_op jit(solution)/shard_map/slice | solution.py:163
  133.8 6.1 %select_reduce_fusion = (f32[2,256]{1,0:T(2,128)S(1)}, f32[2,256,8192]{2,1,0:T(8,128)S(1)}) fusion(pred[256,8192]{1,0:T(8,128)(4,1)S(1)} %copy-done.3, bf16[8192,2,128]{0,2,1:T(8,128)(2,1)} %bitcast.72, bf16[256,2,96]{0,2,1:T(8,128)(2,1)S(1)} %slice.93, bf16[256,2,16]{0,2,1:T(8,128)(2,1)S(1)} %get-tuple-element.16, bf16[256,2,16]{0,2,1:T(8,128)(2,1)S(1)} %get-tuple-element.17), kind=kOutput, calls=%fused_computation.2 | convolution fusion | flops 1086717440 | bytes 23201792 | tf_op jit(solution)/shard_map/qhd,khd->hqk/dot_general | solution.py:63
  139.9 4.8 %fusion = f32[2,256]{1,0:T(2,128)S(1)} fusion(f32[2,256,8192]{2,1,0:T(8,128)S(1)} %get-tuple-element.21, f32[2,256]{1,0:T(2,128)S(1)} %max.7, pred[256,8192]{1,0:T(8,128)(4,1)S(1)} %copy-done.3), kind=kLoop, calls=%fused_computation.3 | loop fusion | flops 16776704 | bytes 18878464 | tf_op jit(solution)/shard_map/reduce_sum | solution.py:74
  145.6 9.4 %fusion.2 = f32[2,256,128]{1,2,0:T(8,128)S(1)} fusion(bf16[8192,2,128]{0,2,1:T(8,128)(2,1)} %bitcast.71, f32[2,256,8192]{2,1,0:T(8,128)} %copy-done.2, f32[2,256]{1,0:T(2,128)S(1)} %max.7, pred[256,8192]{1,0:T(8,128)(4,1)S(1)} %copy-done.3), kind=kOutput, calls=%fused_computation.5 | convolution fusion | flops 1090519040 | bytes 23332864 | tf_op jit(solution)/shard_map/hqk,khd->hqd/dot_general | solution.py:75
  157.8 55.9 %all_to_all.5 = bf16[8,32,4096]{2,1,0:T(8,128)(2,1)} all-to-all(bf16[8,32,4096]{2,1,0:T(8,128)(2,1)S(1)} %bitcast.68), channel_id=1, replica_groups=mesh['seq'=32,'mp'=8] {'mp'}, dimensions={0} | all-to-all | bytes 4194304 | tf_op jit(solution)/shard_map/all_to_all | solution.py:177
  213.7 2.7 %reduce_sum.92 = bf16[32,4096]{1,0:T(8,128)(2,1)} reduce(bf16[8,32,4096]{2,1,0:T(8,128)(2,1)} %all_to_all.5, bf16[]{:T(256)} %constant.90.clone.1), dimensions={0}, to_apply=%region_11.12 | reduce | flops 917504 | bytes 2359298 | tf_op jit(solution)/shard_map/reduce_sum | solution.py:180
  (83 shorter events, 21.2 us)
Async XLA Ops:
  6.5 150.6 %copy-start = (bf16[256,4096]{1,0:T(8,128)(2,1)S(1)}, bf16[256,4096]{1,0:T(8,128)(2,1)}, u32[]{:S(2)}) copy-start(bf16[256,4096]{1,0:T(8,128)(2,1)} %param.16) | copy-start | bytes 6291460
  6.5 16.1 %copy-start.10 = (bf16[4096]{0:T(1024)(128)(2,1)S(1)}, bf16[4096]{0:T(1024)(128)(2,1)}, u32[]{:S(2)}) copy-start(bf16[4096]{0:T(1024)(128)(2,1)} %param.13) | copy-start | bytes 24580
  6.5 16.1 %copy-start.11 = (bf16[4096]{0:T(1024)(128)(2,1)S(1)}, bf16[4096]{0:T(1024)(128)(2,1)}, u32[]{:S(2)}) copy-start(bf16[4096]{0:T(1024)(128)(2,1)} %param.12) | copy-start | bytes 24580
  6.5 121.2 %all-gather.2.cloned.1.call-start = ((), (), s32[]{:S(2)}) async-start(), calls=%async_computation.1 | async-start | bytes 8650752 | tf_op jit(solution)/shard_map/all_gather | solution.py:120
  9.5 28.7 %collective-permute-start = (bf16[256,512]{1,0:T(8,128)(2,1)}, bf16[256,512]{1,0:T(8,128)(2,1)S(1)}, u32[]{:S(2)}, u32[]{:S(2)}) collective-permute-start(bf16[256,512]{1,0:T(8,128)(2,1)} %param.11), channel_id=1, source_target_pairs={{0,1},{1,0},{2,3},{3,2},{4,5},{5,4},{6,7},{7,6},{8,9},{9,8},{10,11... | collective-permute-start | bytes 786440 | tf_op jit(solution)/shard_map/ppermute | solution.py:88
  31.7 6.5 %copy-start.7 = (bf16[256,512]{1,0:T(8,128)(2,1)S(1)}, bf16[256,512]{1,0:T(8,128)(2,1)}, u32[]{:S(2)}) copy-start(bf16[256,512]{1,0:T(8,128)(2,1)} %param.11) | copy-start | bytes 786436
  38.3 25.2 %collective-permute-start.3 = (bf16[256,1024]{1,0:T(8,128)(2,1)S(1)}, bf16[256,1024]{1,0:T(8,128)(2,1)S(1)}, u32[]{:S(2)}, u32[]{:S(2)}) collective-permute-start(bf16[256,1024]{1,0:T(8,128)(2,1)S(1)} %maximum_select_fusion.1), channel_id=1, source_target_pairs={{0,6},{1,7},{2,0},{3,1},{4,2},{5,3},{6,4},{7,5},{8,14},{9,15},{10,... | collective-permute-start | bytes 1572872 | tf_op jit(solution)/shard_map/ppermute | solution.py:97
  41.4 22.2 %collective-permute-start.2 = (bf16[256,1024]{1,0:T(8,128)(2,1)S(1)}, bf16[256,1024]{1,0:T(8,128)(2,1)S(1)}, u32[]{:S(2)}, u32[]{:S(2)}) collective-permute-start(bf16[256,1024]{1,0:T(8,128)(2,1)S(1)} %maximum_select_fusion.1), channel_id=1, source_target_pairs={{0,4},{1,5},{2,6},{3,7},{4,0},{5,1},{6,2},{7,3},{8,12},{9,13},{10,... | collective-permute-start | bytes 1572872 | tf_op jit(solution)/shard_map/ppermute | solution.py:97
  42.0 25.3 %collective-permute-start.1 = (bf16[256,1024]{1,0:T(8,128)(2,1)S(1)}, bf16[256,1024]{1,0:T(8,128)(2,1)S(1)}, u32[]{:S(2)}, u32[]{:S(2)}) collective-permute-start(bf16[256,1024]{1,0:T(8,128)(2,1)S(1)} %maximum_select_fusion.1), channel_id=1, source_target_pairs={{0,2},{1,3},{2,4},{3,5},{4,6},{5,7},{6,0},{7,1},{8,10},{9,11},{10,... | collective-permute-start | bytes 1572872 | tf_op jit(solution)/shard_map/ppermute | solution.py:97
  72.5 2.4 %copy-start.1 = (bf16[4,256,1024]{2,1,0:T(8,128)(2,1)S(1)}, bf16[4,256,1024]{2,1,0:T(8,128)(2,1)}, u32[]{:S(2)}) copy-start(bf16[4,256,1024]{2,1,0:T(8,128)(2,1)} %gather_fusion) | copy-start | bytes 6291460
  81.9 4.4 %copy-start.4 = (bf16[256,4096]{1,0:T(8,128)(2,1)S(1)}, bf16[256,4096]{1,0:T(8,128)(2,1)}, u32[]{:S(2)}) copy-start(bf16[256,4096]{1,0:T(8,128)(2,1)} %copy.61) | copy-start | bytes 6291460
  81.9 4.4 %copy-start.5 = (bf16[256,4,1024]{0,2,1:T(8,128)(2,1)S(1)}, bf16[256,4,1024]{0,2,1:T(8,128)(2,1)}, u32[]{:S(2)}) copy-start(bf16[256,4,1024]{0,2,1:T(8,128)(2,1)} %copy.43) | copy-start | bytes 6291460
  87.1 34.7 %collective-permute-start.4 = (bf16[2,256,2,128]{1,3,2,0:T(8,128)(2,1)S(1)}, bf16[2,256,2,128]{1,3,2,0:T(8,128)(2,1)S(1)}, u32[]{:S(2)}, u32[]{:S(2)}) collective-permute-start(bf16[2,256,2,128]{1,3,2,0:T(8,128)(2,1)S(1)} %pad_maximum_fusion.2), channel_id=1, source_target_pairs={{0,32},{8,40},{16,48},{24,56},{32,64},{40,72},{48,80},{56,88},{64,... | collective-permute-start | bytes 786440 | tf_op jit(solution)/shard_map/ppermute | solution.py:145
  90.5 33.7 %collective-permute-start.5 = (bf16[2,256,2,128]{1,3,2,0:T(8,128)(2,1)S(1)}, bf16[2,256,2,128]{1,3,2,0:T(8,128)(2,1)S(1)}, u32[]{:S(2)}, u32[]{:S(2)}) collective-permute-start(bf16[2,256,2,128]{1,3,2,0:T(8,128)(2,1)S(1)} %pad_maximum_fusion.2), channel_id=1, source_target_pairs={{0,24},{8,32},{16,40},{24,48},{32,56},{40,64},{48,72},{56,80},{64,... | collective-permute-start | bytes 786440 | tf_op jit(solution)/shard_map/ppermute | solution.py:145
  92.8 31.5 %collective-permute-start.6 = (bf16[2,256,2,128]{1,3,2,0:T(8,128)(2,1)S(1)}, bf16[2,256,2,128]{1,3,2,0:T(8,128)(2,1)S(1)}, u32[]{:S(2)}, u32[]{:S(2)}) collective-permute-start(bf16[2,256,2,128]{1,3,2,0:T(8,128)(2,1)S(1)} %pad_maximum_fusion.2), channel_id=1, source_target_pairs={{0,16},{8,24},{16,32},{24,40},{32,48},{40,56},{48,64},{56,72},{64,... | collective-permute-start | bytes 786440 | tf_op jit(solution)/shard_map/ppermute | solution.py:145
  97.0 27.4 %collective-permute-start.7 = (bf16[2,256,2,128]{1,3,2,0:T(8,128)(2,1)S(1)}, bf16[2,256,2,128]{1,3,2,0:T(8,128)(2,1)S(1)}, u32[]{:S(2)}, u32[]{:S(2)}) collective-permute-start(bf16[2,256,2,128]{1,3,2,0:T(8,128)(2,1)S(1)} %pad_maximum_fusion.2), channel_id=1, source_target_pairs={{0,8},{8,16},{16,24},{24,32},{32,40},{40,48},{48,56},{56,64},{64,7... | collective-permute-start | bytes 786440 | tf_op jit(solution)/shard_map/ppermute | solution.py:145
  124.4 1.1 copy-start.8
  127.8 6.0 %copy-start.3 = (pred[256,8192]{1,0:T(8,128)(4,1)S(1)}, pred[256,8192]{1,0:T(8,128)(4,1)}, u32[]{:S(2)}) copy-start(pred[256,8192]{1,0:T(8,128)(4,1)} %broadcast_compare_fusion) | copy-start | bytes 6291460
  139.9 5.7 %copy-start.2 = (f32[2,256,8192]{2,1,0:T(8,128)}, f32[2,256,8192]{2,1,0:T(8,128)S(1)}, u32[]{:S(2)}) copy-start(f32[2,256,8192]{2,1,0:T(8,128)S(1)} %get-tuple-element.21) | copy-start | bytes 50331652
  145.6 9.5 %copy-start.6 = (f32[2,256,1280]{2,1,0:T(8,128)S(1)}, f32[2,256,1280]{2,1,0:T(8,128)}, u32[]{:S(2)}) copy-start(f32[2,256,1280]{2,1,0:T(8,128)} %get-tuple-element.23) | copy-start | bytes 7864324
  155.1 1.3 copy-start.9
Sparse Core Ops, SparseCore 0:
  9.6 93.3 all-gather.1

commit v3 on v2

--- a/solution.py
+++ b/solution.py
@@ -3,7 +3,7 @@
 import jax
 import jax.numpy as jnp
 from jax import lax
-from jax.sharding import PartitionSpec as P
+from jax.sharding import Mesh, PartitionSpec as P
 
 HD = 128
 PBLOCK = 128
@@ -82,22 +82,17 @@
 
 
 def gather_features(tokens):
-    mp_count = lax.psum(1, "mp")
-    ring = mp_count // 2
-    mp_index = lax.axis_index("mp")
-    partner = lax.ppermute(tokens, "mp", [(i, i ^ 1) for i in range(mp_count)])
+    ring = lax.psum(1, "ring")
+    partner = lax.ppermute(tokens, "zh", [(0, 1), (1, 0)])
     pair = jnp.where(
-        mp_index % 2 == 0,
+        lax.axis_index("zh") == 0,
         jnp.concatenate([tokens, partner], 1),
         jnp.concatenate([partner, tokens], 1),
     )
     blocks = [pair]
     for shift in range(1, ring):
-        blocks.append(
-            lax.ppermute(pair, "mp", [(i, (i + 2 * shift) % mp_count) for i in range(mp_count)])
-        )
-    ring_index = mp_index // 2
-    order = (ring_index - jnp.arange(ring, dtype=jnp.int32)) % ring
+        blocks.append(lax.ppermute(pair, "ring", [(i, (i + shift) % ring) for i in range(ring)]))
+    order = (lax.axis_index("ring") - jnp.arange(ring, dtype=jnp.int32)) % ring
     stacked = jnp.stack(blocks, 0)[order]
     return stacked.transpose(1, 0, 2).reshape(tokens.shape[0], -1)
 
@@ -117,15 +112,26 @@
 ):
     prefix_rows = prefix_key.shape[0]
     local_heads = w_query.shape[1] // HD
-    prefix_both = lax.all_gather(
-        jnp.stack([prefix_key, prefix_value], 0), "seq", axis=1, tiled=True
-    )
+    core_index = lax.axis_index("core")
+    first_core = core_index == 0
+    kept = jnp.where(first_core, prefix_key, prefix_value)
+    given = jnp.where(first_core, prefix_value, prefix_key)
+    received = lax.ppermute(given, "core", [(0, 1), (1, 0)])
+    chip_rows = jnp.where(
+        first_core,
+        jnp.concatenate([kept, received], 0),
+        jnp.concatenate([received, kept], 0),
+    )
+    gathered_half = lax.all_gather(chip_rows, "chip", axis=0, tiled=True)
+    other_half = lax.ppermute(gathered_half, "core", [(0, 1), (1, 0)])
+    prefix_k_all = jnp.where(first_core, gathered_half, other_half)
+    prefix_v_all = jnp.where(first_core, other_half, gathered_half)
     gathered = gather_features(tokens)
     token_count = gathered.shape[0]
     feature_count = gathered.shape[1]
     normed = layer_norm(gathered, norm_gain, norm_bias)
-    seq_index = lax.axis_index("seq")
-    seq_count = lax.psum(1, "seq")
+    seq_index = lax.axis_index(SEQ)
+    seq_count = lax.psum(1, SEQ)
     global_index = seq_index * token_count + jnp.arange(token_count, dtype=jnp.int32)
     request, cached_len, position = request_info(global_index, lengths, context)
     query_raw = jnp.dot(normed, w_query, preferred_element_type=jnp.float32).reshape(
@@ -142,7 +148,7 @@
     window = [key_value]
     for shift in range(1, SUFFIX_SHARDS):
         pairs = [(i, i + shift) for i in range(seq_count - shift)]
-        window.insert(0, lax.ppermute(key_value, "seq", pairs))
+        window.insert(0, lax.ppermute(key_value, SEQ, pairs))
     window = jnp.concatenate(window, 1)
     window_count = window.shape[1]
     key_index = (seq_index - (SUFFIX_SHARDS - 1)) * token_count + jnp.arange(
@@ -155,13 +161,13 @@
         & (key_index[None, :] <= global_index[:, None])
     )
 
-    prefix_all = prefix_both.shape[1]
+    prefix_all = prefix_k_all.shape[0]
     prefix_position = (
         prefix_place[:, None] * PBLOCK + jnp.arange(PBLOCK, dtype=jnp.int32)[None, :]
     ).reshape(-1)
     sees_prefix = prefix_position[None, :] < cached_len[:, None]
-    prefix_keys = prefix_both[0].reshape(prefix_all, local_heads, HD)
-    prefix_values = prefix_both[1].reshape(prefix_all, local_heads, HD)
+    prefix_keys = prefix_k_all.reshape(prefix_all, local_heads, HD)
+    prefix_values = prefix_v_all.reshape(prefix_all, local_heads, HD)
 
     attended = masked_softmax_attention(
         queries,
@@ -173,30 +179,43 @@
         attended.astype(jnp.bfloat16).transpose(1, 0, 2).reshape(token_count, local_heads * HD)
     )
     partial = jnp.dot(heads_out, w_out, preferred_element_type=jnp.float32).astype(jnp.bfloat16)
-    mp_count = lax.psum(1, "mp")
-    exchanged = lax.all_to_all(
-        partial.reshape(mp_count, token_count // mp_count, -1), "mp", 0, 0, tiled=False
-    )
-    return jnp.sum(exchanged.astype(jnp.float32), 0).astype(jnp.bfloat16)
+    ring = lax.psum(1, "ring")
+    pairs = lax.psum(1, "zh")
+    by_ring = lax.all_to_all(
+        partial.reshape(ring, token_count // ring, -1), "ring", 0, 0, tiled=False
+    )
+    ring_sum = jnp.sum(by_ring.astype(jnp.float32), 0)
+    by_pair = lax.all_to_all(
+        ring_sum.reshape(pairs, token_count // (ring * pairs), -1), "zh", 0, 0, tiled=False
+    )
+    return jnp.sum(by_pair, 0).astype(jnp.bfloat16)
+
+
+SEQ = ("chip", "core")
+MP = ("ring", "zh")
 
 
 def solution(mesh):
+    seq_count, mp_count = mesh.devices.shape
+    split_mesh = Mesh(
+        mesh.devices.reshape(seq_count // 2, 2, mp_count // 2, 2), ("chip", "core", "ring", "zh")
+    )
     return jax.shard_map(
         body,
-        mesh=mesh,
+        mesh=split_mesh,
         in_specs=(
-            P("seq", "mp"),
-            P(),
-            P(),
-            P(None, "mp"),
-            P(None, None, "mp"),
-            P("mp", None),
-            P("seq", "mp"),
-            P("seq", "mp"),
+            P(SEQ, MP),
+            P(),
+            P(),
+            P(None, MP),
+            P(None, None, MP),
+            P(MP, None),
+            P(SEQ, MP),
+            P(SEQ, MP),
             P(),
             P(),
             P(),
         ),
-        out_specs=P(("seq", "mp"), None),
+        out_specs=P(SEQ + MP, None),
         check_vma=False,
     )

time: 227 us -> 271 us (1.19)
  waiting for transfers between devices: 48.3 us -> 86.8 us
  other arithmetic: 21.8 us -> 28.1 us
    all_gather x1, waiting for transfers between devices: 0.01 us -> 42.1 us  [body(): gathered_half = lax.all_gather(chip_rows, 'chip', axis=0, tiled=True)]
    select_n x2 -> x5, other arithmetic: 0.26 us -> 7.33 us  [the longest x1 5.12 us: body(): prefix_v_all = jnp.where(first_core, other_half, gathered_half)]
    reshape x0 -> x1, local copies, waits for them, and re-layouts: none -> 6.41 us  [body(): prefix_values = prefix_v_all.reshape(prefix_all, local_heads, HD)]
    slice x1 -> x0, local copies, waits for them, and re-layouts: 6.03 us -> none  [body(): prefix_keys = prefix_both[0].reshape(prefix_all, local_heads, HD)]
    ppermute x8 -> x10, waiting for transfers between devices: 48.3 us -> 44.7 us  [the longest x4 22.1 us: body(): window.insert(0, lax.ppermute(key_value, SEQ, pairs))]
    all_to_all x1 -> x2, blocking collectives: 55.9 us -> 57.1 us  [the longest x1 29 us: body(): lax.all_to_all(ring_sum.reshape(pairs, token_count // (ring * pairs), -1)...]
    ppermute x8 -> x10, starting transfers between devices: 24.3 us -> 25.3 us  [the longest x4 12 us: body(): window.insert(0, lax.ppermute(key_value, SEQ, pairs))]
  transfers between devices with their start and end apart: 9 -> 11, of which waited for: 4 -> 6; matrix products, arithmetic and copies ran while one was open for 20% -> 16% of each run, Pallas kernels for 0% -> 0%
where the time goes in v3:
time: 271 us; the launch traced here: 270 us
  waiting for transfers between devices  86.8 us (32%)
  blocking collectives  57.1 us (21%)
  local copies, waits for them, and re-layouts  33.6 us (12%)
  other arithmetic  28.1 us (10%)
  starting transfers between devices  25.3 us (9%)
  matrix products  25 us (9%)
  between operations  13.8 us (5%)
    all_gather x1, waiting for transfers between devices, body(): gathered_half = lax.all_gather(chip_rows, 'chip', axis=0, tiled=True)  42.1 us
    all_to_all x1, blocking collectives, body(): lax.all_to_all(ring_sum.reshape(pairs, token_count // (ring * pairs), -1)...  29 us
    all_to_all x1, blocking collectives, body(): lax.all_to_all(partial.reshape(ring, token_count // ring, -1), 'ring', 0,...  28 us
    ppermute x4, waiting for transfers between devices, body(): window.insert(0, lax.ppermute(key_value, SEQ, pairs))  22.1 us
    ppermute x3, waiting for transfers between devices, gather_features(): lax.ppermute(pair, 'ring', [(i, (i + shift) % ring) for i in range(ring)])  21.3 us
    dot_general x2, matrix products, masked_softmax_attention(): jnp.einsum('hqk,khd->hqd', probs.astype(jnp.bfloat16), values, preferred_...  12.5 us
    ppermute x4, starting transfers between devices, body(): window.insert(0, lax.ppermute(key_value, SEQ, pairs))  12 us
    unnamed x31, local copies, waits for them, and re-layouts  8.28 us
  transfers between devices with their start and end apart: 11, of which 6 were waited for; matrix products, arithmetic and copies ran while one was open for 16% of the time, Pallas kernels for 0%

profile of v3, /device:TPU:2, one launch (start us, length us, event | category | flops | bytes accessed | tf_op | source)
XLA Modules:
  0.0 269.8 jit_solution(17530148566626282143)
XLA Ops:
  10.0 7.3 %collective-permute-start = (bf16[256,512]{1,0:T(8,128)(2,1)}, bf16[256,512]{1,0:T(8,128)(2,1)S(1)}, u32[]{:S(2)}, u32[]{:S(2)}) collective-permute-start(bf16[256,512]{1,0:T(8,128)(2,1)} %param.11), channel_id=1, source_target_pairs={{0,1},{1,0},{2,3},{3,2},{4,5},{5,4},{6,7},{7,6},{8,9},{9,8},{10,11... | collective-permute-start | bytes 786440 | tf_op jit(solution)/shard_map/ppermute | solution.py:86
  20.5 2.6 broadcast_compare_fusion
  23.1 5.0 %copy.62 = bf16[512,8,2,256]{3,1,2,0:T(8,128)(2,1)} copy(bf16[512,8,2,256]{3,2,1,0:T(2,128)(2,1)} %bitcast.74) | data formatting | bytes 8388608
  28.1 6.4 %copy.47 = bf16[512,4096]{1,0:T(8,128)(2,1)} copy(bf16[512,4096]{0,1:T(8,128)(2,1)} %bitcast.68) | data formatting | bytes 8388608 | tf_op jit(solution)/shard_map/dot_general | solution.py:140
  34.5 4.1 %copy.58 = bf16[256,4096]{1,0:T(8,128)(2,1)} copy(bf16[256,4096]{0,1:T(8,128)(2,1)} %bitcast.77) | data formatting | bytes 4194304 | tf_op jit(solution)/shard_map/dot_general | solution.py:137
  40.5 2.9 %collective-permute-start.2 = (bf16[256,1024]{1,0:T(8,128)(2,1)S(1)}, bf16[256,1024]{1,0:T(8,128)(2,1)S(1)}, u32[]{:S(2)}, u32[]{:S(2)}) collective-permute-start(bf16[256,1024]{1,0:T(8,128)(2,1)S(1)} %maximum_select_fusion.1), channel_id=1, source_target_pairs={{0,4},{2,6},{4,0},{6,2},{1,5},{3,7},{5,1},{7,3},{8,12},{10,14},{12... | collective-permute-start | bytes 1572872 | tf_op jit(solution)/shard_map/ppermute | solution.py:94
  45.0 8.9 %collective-permute-done.1 = bf16[256,1024]{1,0:T(8,128)(2,1)S(1)} collective-permute-done((bf16[256,1024]{1,0:T(8,128)(2,1)S(1)}, bf16[256,1024]{1,0:T(8,128)(2,1)S(1)}, u32[]{:S(2)}, u32[]{:S(2)}) %collective-permute-start.1) | collective-permute-done | bytes 524320 | tf_op jit(solution)/shard_map/ppermute | solution.py:94
  53.9 12.4 %collective-permute-done.2 = bf16[256,1024]{1,0:T(8,128)(2,1)S(1)} collective-permute-done((bf16[256,1024]{1,0:T(8,128)(2,1)S(1)}, bf16[256,1024]{1,0:T(8,128)(2,1)S(1)}, u32[]{:S(2)}, u32[]{:S(2)}) %collective-permute-start.2) | collective-permute-done | bytes 524320 | tf_op jit(solution)/shard_map/ppermute | solution.py:94
  67.9 3.6 %gather_fusion = bf16[4,256,1024]{2,1,0:T(8,128)(2,1)} fusion(bf16[4,256,1024]{2,1,0:T(8,128)(2,1)} %pad_maximum_fusion, s32[1024]{0:T(1024)S(1)} %pad_clamp_fusion), kind=kCustom, calls=%fused_computation | custom fusion | bytes 4194320 | tf_op jit(solution)/shard_map/gather | solution.py:96
  73.5 42.1 %all-gather.2.cloned.1.call-done = bf16[8192,256]{1,0:T(8,128)(2,1)} async-done(((bf16[512,256]{1,0:T(8,128)(2,1)}), bf16[8192,256]{1,0:T(8,128)(2,1)}) %all-gather.2.cloned.1.call-update) | async-done | bytes 4194320 | tf_op jit(solution)/shard_map/all_gather | solution.py:125
  120.4 3.9 %copy.42 = bf16[256,4,1024]{0,2,1:T(8,128)(2,1)} copy(bf16[256,4,1024]{2,0,1:T(8,128)(2,1)} %fusion.16) | data formatting | bytes 4194304 | tf_op jit(solution)/shard_map/convert_element_type | solution.py:21
  124.4 4.2 %fusion.47 = f32[256,2,2,128]{0,3,2,1:T(8,128)S(1)} fusion(bf16[256,4096,1,1]{0,1,3,2:T(8,128)(2,1)} %bitcast.70, bf16[2,2,128,4096]{3,2,1,0:T(8,128)(2,1)} %bitcast.75), kind=kOutput, calls=%fused_computation.99 | convolution fusion | flops 1073741824 | bytes 6815744 | tf_op jit(solution)/shard_map/dot_general | solution.py:140
  129.5 2.7 %collective-permute-start.6 = (bf16[2,256,2,128]{1,3,2,0:T(8,128)(2,1)S(1)}, bf16[2,256,2,128]{1,3,2,0:T(8,128)(2,1)S(1)}, u32[]{:S(2)}, u32[]{:S(2)}) collective-permute-start(bf16[2,256,2,128]{1,3,2,0:T(8,128)(2,1)S(1)} %pad_maximum_fusion.1), channel_id=1, source_target_pairs={{0,32},{8,40},{16,48},{24,56},{32,64},{40,72},{48,80},{56,88},{64,... | collective-permute-start | bytes 786440 | tf_op jit(solution)/shard_map/ppermute | solution.py:151
  132.2 4.7 %collective-permute-start.7 = (bf16[2,256,2,128]{1,3,2,0:T(8,128)(2,1)S(1)}, bf16[2,256,2,128]{1,3,2,0:T(8,128)(2,1)S(1)}, u32[]{:S(2)}, u32[]{:S(2)}) collective-permute-start(bf16[2,256,2,128]{1,3,2,0:T(8,128)(2,1)S(1)} %pad_maximum_fusion.1), channel_id=1, source_target_pairs={{0,24},{8,32},{16,40},{24,48},{32,56},{40,64},{48,72},{56,80},{64,... | collective-permute-start | bytes 786440 | tf_op jit(solution)/shard_map/ppermute | solution.py:151
  136.8 2.8 %collective-permute-start.8 = (bf16[2,256,2,128]{1,3,2,0:T(8,128)(2,1)S(1)}, bf16[2,256,2,128]{1,3,2,0:T(8,128)(2,1)S(1)}, u32[]{:S(2)}, u32[]{:S(2)}) collective-permute-start(bf16[2,256,2,128]{1,3,2,0:T(8,128)(2,1)S(1)} %pad_maximum_fusion.1), channel_id=1, source_target_pairs={{0,16},{8,24},{16,32},{24,40},{32,48},{40,56},{48,64},{56,72},{64,... | collective-permute-start | bytes 786440 | tf_op jit(solution)/shard_map/ppermute | solution.py:151
  142.0 19.3 %collective-permute-done.6 = bf16[2,256,2,128]{1,3,2,0:T(8,128)(2,1)S(1)} collective-permute-done((bf16[2,256,2,128]{1,3,2,0:T(8,128)(2,1)S(1)}, bf16[2,256,2,128]{1,3,2,0:T(8,128)(2,1)S(1)}, u32[]{:S(2)}, u32[]{:S(2)}) %collective-permute-start.6) | collective-permute-done | bytes 262176 | tf_op jit(solution)/shard_map/ppermute | solution.py:151
  161.3 2.7 %collective-permute-done.7 = bf16[2,256,2,128]{1,3,2,0:T(8,128)(2,1)S(1)} collective-permute-done((bf16[2,256,2,128]{1,3,2,0:T(8,128)(2,1)S(1)}, bf16[2,256,2,128]{1,3,2,0:T(8,128)(2,1)S(1)}, u32[]{:S(2)}, u32[]{:S(2)}) %collective-permute-start.7) | collective-permute-done | bytes 262176 | tf_op jit(solution)/shard_map/ppermute | solution.py:151
  166.8 5.1 %broadcast_select_fusion = (bf16[8192,256]{1,0:T(8,128)(2,1)}, bf16[1024,2,8,128]{3,2,1,0:T(8,128)(2,1)}) fusion(bf16[8192,256]{1,0:T(8,128)(2,1)} %collective-permute-done.5, bf16[8192,256]{1,0:T(8,128)(2,1)S(1)} %copy-done.6, pred[]{:T(512)S(6)} %eq.26), kind=kLoop, calls=%fused_computation.22 | loop fusion | flops 4194304 | bytes 16777216 | tf_op jit(solution)/shard_map/jit(_where)/select_n | solution.py:128
  171.9 6.0 %select_reduce_fusion = (f32[2,256]{1,0:T(2,128)S(1)}, f32[2,256,8192]{2,1,0:T(8,128)S(1)}) fusion(pred[256,8192]{1,0:T(8,128)(4,1)S(1)} %copy-done.3, bf16[1024,2,8,128]{3,2,1,0:T(8,128)(2,1)} %get-tuple-element.11, bf16[256,2,96]{0,2,1:T(8,128)(2,1)S(1)} %slice.83, bf16[256,2,16]{0,2,1:T(8,128)(2,1)S(1)} %get-tuple-element.13, ...), kind=kOutput, calls=%fused_computation.2 | convolution fusion | flops 1086717440 | bytes 23201792 | tf_op jit(solution)/shard_map/qhd,khd->hqk/dot_general | solution.py:63
  182.5 4.8 %fusion = f32[2,256]{1,0:T(2,128)S(1)} fusion(f32[2,256,8192]{2,1,0:T(8,128)S(1)} %get-tuple-element.23, f32[2,256]{1,0:T(2,128)S(1)} %max.7, pred[256,8192]{1,0:T(8,128)(4,1)S(1)} %copy-done.3), kind=kLoop, calls=%fused_computation.3 | loop fusion | flops 16776704 | bytes 18878464 | tf_op jit(solution)/shard_map/reduce_sum | solution.py:74
  187.3 6.4 %copy.60 = bf16[8192,256]{0,1:T(8,128)(2,1)} copy(bf16[8192,256]{1,0:T(8,128)(2,1)} %get-tuple-element.10) | data formatting | bytes 8388608 | tf_op jit(solution)/shard_map/reshape | solution.py:170
  193.7 10.3 %fusion.31 = bf16[256,2,128]{0,2,1:T(8,128)(2,1)S(1)} fusion(f32[2,256,128]{1,2,0:T(8,128)S(1)} %copy-done.12, bf16[8192,2,128]{0,2,1:T(8,128)(2,1)} %bitcast.76, f32[2,256,8192]{2,1,0:T(8,128)} %copy-done.2, f32[2,256]{1,0:T(2,128)S(1)} %max.7, pred[256,8192]{1,0:T(8,128)(4,1)} %broadcast_compare_fusion, f32[256,2]{0,1:T(2,128)S(1)} %add_bitcast_fusion.1), kind=kOutput, calls=%fused_computation.38 | convolution fusion | flops 1090715648 | bytes 23465984 | tf_op jit(solution)/shard_map/hqk,khd->hqd/dot_general | solution.py:75
  204.7 28.0 %all_to_all.10 = bf16[4,64,4096]{2,1,0:T(8,128)(2,1)S(1)} all-to-all(bf16[4,64,4096]{2,1,0:T(8,128)(2,1)S(1)} %bitcast.72), channel_id=1, replica_groups=mesh['chip'=16,'core'=2,'ring'=4,'zh'=2] {'ring'}, dimensions={0} | all-to-all | bytes 4194304 | tf_op jit(solution)/shard_map/all_to_all | solution.py:184
  233.1 29.0 %all_to_all.11 = f32[2,32,4096]{2,1,0:T(8,128)S(1)} all-to-all(f32[2,32,4096]{2,1,0:T(8,128)S(1)} %bitcast.73), channel_id=1, replica_groups=mesh['chip'=16,'core'=2,'ring'=4,'zh'=2] {'zh'}, dimensions={0} | all-to-all | bytes 2097152 | tf_op jit(solution)/shard_map/all_to_all | solution.py:188
  (91 shorter events, 30.6 us)
Async XLA Ops:
  6.5 197.5 %copy-start = (bf16[256,4096]{1,0:T(8,128)(2,1)S(1)}, bf16[256,4096]{1,0:T(8,128)(2,1)}, u32[]{:S(2)}) copy-start(bf16[256,4096]{1,0:T(8,128)(2,1)} %param.16) | copy-start | bytes 6291460
  6.5 16.6 %copy-start.10 = (bf16[4096]{0:T(1024)(128)(2,1)S(1)}, bf16[4096]{0:T(1024)(128)(2,1)}, u32[]{:S(2)}) copy-start(bf16[4096]{0:T(1024)(128)(2,1)} %param.12) | copy-start | bytes 24580
  6.5 16.6 %copy-start.11 = (bf16[4096]{0:T(1024)(128)(2,1)S(1)}, bf16[4096]{0:T(1024)(128)(2,1)}, u32[]{:S(2)}) copy-start(bf16[4096]{0:T(1024)(128)(2,1)} %param.13) | copy-start | bytes 24580
  6.5 109.0 %all-gather.2.cloned.1.call-start = ((), (), s32[]{:S(2)}) async-start(), calls=%async_computation.2 | async-start | bytes 4456448 | tf_op jit(solution)/shard_map/all_gather | solution.py:125
  7.7 1.4 collective-permute-start.4
  10.0 28.7 %collective-permute-start = (bf16[256,512]{1,0:T(8,128)(2,1)}, bf16[256,512]{1,0:T(8,128)(2,1)S(1)}, u32[]{:S(2)}, u32[]{:S(2)}) collective-permute-start(bf16[256,512]{1,0:T(8,128)(2,1)} %param.11), channel_id=1, source_target_pairs={{0,1},{1,0},{2,3},{3,2},{4,5},{5,4},{6,7},{7,6},{8,9},{9,8},{10,11... | collective-permute-start | bytes 786440 | tf_op jit(solution)/shard_map/ppermute | solution.py:86
  34.5 4.2 %copy-start.7 = (bf16[256,512]{1,0:T(8,128)(2,1)S(1)}, bf16[256,512]{1,0:T(8,128)(2,1)}, u32[]{:S(2)}) copy-start(bf16[256,512]{1,0:T(8,128)(2,1)} %param.11) | copy-start | bytes 786436
  38.8 15.1 %collective-permute-start.1 = (bf16[256,1024]{1,0:T(8,128)(2,1)S(1)}, bf16[256,1024]{1,0:T(8,128)(2,1)S(1)}, u32[]{:S(2)}, u32[]{:S(2)}) collective-permute-start(bf16[256,1024]{1,0:T(8,128)(2,1)S(1)} %maximum_select_fusion.1), channel_id=1, source_target_pairs={{0,2},{2,4},{4,6},{6,0},{1,3},{3,5},{5,7},{7,1},{8,10},{10,12},{12... | collective-permute-start | bytes 1572872 | tf_op jit(solution)/shard_map/ppermute | solution.py:94
  40.5 25.8 %collective-permute-start.2 = (bf16[256,1024]{1,0:T(8,128)(2,1)S(1)}, bf16[256,1024]{1,0:T(8,128)(2,1)S(1)}, u32[]{:S(2)}, u32[]{:S(2)}) collective-permute-start(bf16[256,1024]{1,0:T(8,128)(2,1)S(1)} %maximum_select_fusion.1), channel_id=1, source_target_pairs={{0,4},{2,6},{4,0},{6,2},{1,5},{3,7},{5,1},{7,3},{8,12},{10,14},{12... | collective-permute-start | bytes 1572872 | tf_op jit(solution)/shard_map/ppermute | solution.py:94
  43.4 22.9 %collective-permute-start.3 = (bf16[256,1024]{1,0:T(8,128)(2,1)S(1)}, bf16[256,1024]{1,0:T(8,128)(2,1)S(1)}, u32[]{:S(2)}, u32[]{:S(2)}) collective-permute-start(bf16[256,1024]{1,0:T(8,128)(2,1)S(1)} %maximum_select_fusion.1), channel_id=1, source_target_pairs={{0,6},{2,0},{4,2},{6,4},{1,7},{3,1},{5,3},{7,5},{8,14},{10,8},{12,... | collective-permute-start | bytes 1572872 | tf_op jit(solution)/shard_map/ppermute | solution.py:94
  115.6 2.5 copy-start.1
  115.6 50.6 %collective-permute-start.5 = (bf16[8192,256]{1,0:T(8,128)(2,1)}, bf16[8192,256]{1,0:T(8,128)(2,1)}, u32[]{:S(2)}, u32[]{:S(2)}) collective-permute-start(bf16[8192,256]{1,0:T(8,128)(2,1)} %all-gather.2.cloned.1.call-done), channel_id=1, source_target_pairs={{0,8},{8,0},{1,9},{9,1},{2,10},{10,2},{3,11},{11,3},{4,12},{12,4},... | collective-permute-start | bytes 12582920 | tf_op jit(solution)/shard_map/ppermute | solution.py:126
  124.4 4.3 %copy-start.4 = (bf16[256,4096]{1,0:T(8,128)(2,1)S(1)}, bf16[256,4096]{1,0:T(8,128)(2,1)}, u32[]{:S(2)}) copy-start(bf16[256,4096]{1,0:T(8,128)(2,1)} %copy.58) | copy-start | bytes 6291460
  124.4 4.3 %copy-start.5 = (bf16[256,4,1024]{0,2,1:T(8,128)(2,1)S(1)}, bf16[256,4,1024]{0,2,1:T(8,128)(2,1)}, u32[]{:S(2)}) copy-start(bf16[256,4,1024]{0,2,1:T(8,128)(2,1)} %copy.42) | copy-start | bytes 6291460
  129.5 31.8 %collective-permute-start.6 = (bf16[2,256,2,128]{1,3,2,0:T(8,128)(2,1)S(1)}, bf16[2,256,2,128]{1,3,2,0:T(8,128)(2,1)S(1)}, u32[]{:S(2)}, u32[]{:S(2)}) collective-permute-start(bf16[2,256,2,128]{1,3,2,0:T(8,128)(2,1)S(1)} %pad_maximum_fusion.1), channel_id=1, source_target_pairs={{0,32},{8,40},{16,48},{24,56},{32,64},{40,72},{48,80},{56,88},{64,... | collective-permute-start | bytes 786440 | tf_op jit(solution)/shard_map/ppermute | solution.py:151
  132.2 31.9 %collective-permute-start.7 = (bf16[2,256,2,128]{1,3,2,0:T(8,128)(2,1)S(1)}, bf16[2,256,2,128]{1,3,2,0:T(8,128)(2,1)S(1)}, u32[]{:S(2)}, u32[]{:S(2)}) collective-permute-start(bf16[2,256,2,128]{1,3,2,0:T(8,128)(2,1)S(1)} %pad_maximum_fusion.1), channel_id=1, source_target_pairs={{0,24},{8,32},{16,40},{24,48},{32,56},{40,64},{48,72},{56,80},{64,... | collective-permute-start | bytes 786440 | tf_op jit(solution)/shard_map/ppermute | solution.py:151
  136.8 27.3 %collective-permute-start.8 = (bf16[2,256,2,128]{1,3,2,0:T(8,128)(2,1)S(1)}, bf16[2,256,2,128]{1,3,2,0:T(8,128)(2,1)S(1)}, u32[]{:S(2)}, u32[]{:S(2)}) collective-permute-start(bf16[2,256,2,128]{1,3,2,0:T(8,128)(2,1)S(1)} %pad_maximum_fusion.1), channel_id=1, source_target_pairs={{0,16},{8,24},{16,32},{24,40},{32,48},{40,56},{48,64},{56,72},{64,... | collective-permute-start | bytes 786440 | tf_op jit(solution)/shard_map/ppermute | solution.py:151
  140.1 24.1 %collective-permute-start.9 = (bf16[2,256,2,128]{1,3,2,0:T(8,128)(2,1)S(1)}, bf16[2,256,2,128]{1,3,2,0:T(8,128)(2,1)S(1)}, u32[]{:S(2)}, u32[]{:S(2)}) collective-permute-start(bf16[2,256,2,128]{1,3,2,0:T(8,128)(2,1)S(1)} %pad_maximum_fusion.1), channel_id=1, source_target_pairs={{0,8},{8,16},{16,24},{24,32},{32,40},{40,48},{48,56},{56,64},{64,7... | collective-permute-start | bytes 786440 | tf_op jit(solution)/shard_map/ppermute | solution.py:151
  164.1 2.7 copy-start.6
  164.2 1.1 copy-start.8
  166.1 5.8 %copy-start.3 = (pred[256,8192]{1,0:T(8,128)(4,1)S(1)}, pred[256,8192]{1,0:T(8,128)(4,1)}, u32[]{:S(2)}) copy-start(pred[256,8192]{1,0:T(8,128)(4,1)} %broadcast_compare_fusion) | copy-start | bytes 6291460
  177.9 9.3 %copy-start.2 = (f32[2,256,8192]{2,1,0:T(8,128)}, f32[2,256,8192]{2,1,0:T(8,128)S(1)}, u32[]{:S(2)}) copy-start(f32[2,256,8192]{2,1,0:T(8,128)S(1)} %get-tuple-element.23) | copy-start | bytes 50331652
  177.9 2.3 copy-start.9
  187.2 6.4 %copy-start.12 = (f32[2,256,128]{1,2,0:T(8,128)S(1)}, f32[2,256,128]{1,2,0:T(8,128)}, u32[]{:S(2)}) copy-start(f32[2,256,128]{1,2,0:T(8,128)} %fusion.17) | copy-start | bytes 786436
Sparse Core Ops, SparseCore 0:
  10.1 105.4 all-gather.1

commit v4 on v2

--- a/solution.py
+++ b/solution.py
@@ -117,8 +117,8 @@
 ):
     prefix_rows = prefix_key.shape[0]
     local_heads = w_query.shape[1] // HD
-    prefix_both = lax.all_gather(
-        jnp.stack([prefix_key, prefix_value], 0), "seq", axis=1, tiled=True
+    prefix_k_all, prefix_v_all = lax.all_gather(
+        (prefix_key, prefix_value), "seq", axis=0, tiled=True
     )
     gathered = gather_features(tokens)
     token_count = gathered.shape[0]
@@ -155,13 +155,13 @@
         & (key_index[None, :] <= global_index[:, None])
     )
 
-    prefix_all = prefix_both.shape[1]
+    prefix_all = prefix_k_all.shape[0]
     prefix_position = (
         prefix_place[:, None] * PBLOCK + jnp.arange(PBLOCK, dtype=jnp.int32)[None, :]
     ).reshape(-1)
     sees_prefix = prefix_position[None, :] < cached_len[:, None]
-    prefix_keys = prefix_both[0].reshape(prefix_all, local_heads, HD)
-    prefix_values = prefix_both[1].reshape(prefix_all, local_heads, HD)
+    prefix_keys = prefix_k_all.reshape(prefix_all, local_heads, HD)
+    prefix_values = prefix_v_all.reshape(prefix_all, local_heads, HD)
 
     attended = masked_softmax_attention(
         queries,

time: 227 us -> 253 us (1.11)
  waiting for transfers between devices: 48.3 us -> 67 us
  local copies, waits for them, and re-layouts: 34.8 us -> 39.7 us
  blocking collectives: 55.9 us -> 60.2 us
    all_gather x1 -> x2, waiting for transfers between devices: 0.01 us -> 13.7 us  [body(): lax.all_gather((prefix_key, prefix_value), 'seq', axis=0, tiled=True)]
    all_gather x0 -> x1, local copies, waits for them, and re-layouts: none -> 6.36 us  [body(): lax.all_gather((prefix_key, prefix_value), 'seq', axis=0, tiled=True)]
    slice x1 -> x0, local copies, waits for them, and re-layouts: 6.03 us -> none  [body(): prefix_keys = prefix_both[0].reshape(prefix_all, local_heads, HD)]
    ppermute x4, waiting for transfers between devices: 24.3 us -> 29.4 us  [body(): window.insert(0, lax.ppermute(key_value, 'seq', pairs))]
    unnamed x31 -> x30, local copies, waits for them, and re-layouts: 9.83 us -> 14.2 us
    all_to_all x1, blocking collectives: 55.9 us -> 60.2 us  [body(): lax.all_to_all(partial.reshape(mp_count, token_count // mp_count, -1), 'm...]
  transfers between devices with their start and end apart: 9 -> 10, of which waited for: 4 -> 5; matrix products, arithmetic and copies ran while one was open for 20% -> 22% of each run, Pallas kernels for 0% -> 0%
where the time goes in v4:
time: 253 us; the launch traced here: 251 us
  waiting for transfers between devices  67 us (26%)
  blocking collectives  60.2 us (24%)
  local copies, waits for them, and re-layouts  39.7 us (16%)
  matrix products  25.2 us (10%)
  starting transfers between devices  24.5 us (10%)
  other arithmetic  21 us (8%)
  between operations  13.8 us (5%)
    all_to_all x1, blocking collectives, body(): lax.all_to_all(partial.reshape(mp_count, token_count // mp_count, -1), 'm...  60.2 us
    ppermute x4, waiting for transfers between devices, body(): window.insert(0, lax.ppermute(key_value, 'seq', pairs))  29.4 us
    ppermute x3, waiting for transfers between devices, gather_features(): lax.ppermute(pair, 'mp', [(i, (i + 2 * shift) % mp_count) for i in range(...  23.9 us
    unnamed x30, local copies, waits for them, and re-layouts  14.2 us
    all_gather x2, waiting for transfers between devices, body(): lax.all_gather((prefix_key, prefix_value), 'seq', axis=0, tiled=True)  13.7 us
    ppermute x4, starting transfers between devices, body(): window.insert(0, lax.ppermute(key_value, 'seq', pairs))  12.4 us
    dot_general x2, matrix products, masked_softmax_attention(): jnp.einsum('hqk,khd->hqd', probs.astype(jnp.bfloat16), values, preferred_...  10.7 us
    dot_general x2, matrix products, masked_softmax_attention(): jnp.einsum('qhd,khd->hqk', queries, keys, preferred_element_type=jnp.floa...  8.83 us
  transfers between devices with their start and end apart: 10, of which 5 were waited for; matrix products, arithmetic and copies ran while one was open for 22% of the time, Pallas kernels for 0%

profile of v4, /device:TPU:2, one launch (start us, length us, event | category | flops | bytes accessed | tf_op | source)
XLA Modules:
  0.0 251.4 jit_solution(8779595677883809515)
XLA Ops:
  8.4 7.3 %collective-permute-start = (bf16[256,512]{1,0:T(8,128)(2,1)}, bf16[256,512]{1,0:T(8,128)(2,1)S(1)}, u32[]{:S(2)}, u32[]{:S(2)}) collective-permute-start(bf16[256,512]{1,0:T(8,128)(2,1)} %param.11), channel_id=1, source_target_pairs={{0,1},{1,0},{2,3},{3,2},{4,5},{5,4},{6,7},{7,6},{8,9},{9,8},{10,11... | collective-permute-start | bytes 786440 | tf_op jit(solution)/shard_map/ppermute | solution.py:88
  19.0 2.6 %broadcast_compare_fusion = pred[256,8192]{1,0:T(8,128)(4,1)} fusion(s32[8192]{0:T(1024)S(1)} %add_bitcast_fusion, s32[256]{0:T(256)S(1)} %get-tuple-element.7), kind=kLoop, calls=%fused_computation.16 | loop fusion | flops 2097152 | bytes 2130944 | tf_op jit(solution)/shard_map/lt | solution.py:162
  21.6 4.1 %copy.61 = bf16[256,4096]{1,0:T(8,128)(2,1)} copy(bf16[256,4096]{0,1:T(8,128)(2,1)} %bitcast.70) | data formatting | bytes 4194304 | tf_op jit(solution)/shard_map/dot_general | solution.py:131
  25.8 4.9 %copy.63 = bf16[512,8,2,256]{3,1,2,0:T(8,128)(2,1)} copy(bf16[512,8,2,256]{3,2,1,0:T(2,128)(2,1)} %bitcast.67) | data formatting | bytes 8388608
  30.7 6.5 %copy.49 = bf16[512,4096]{1,0:T(8,128)(2,1)} copy(bf16[512,4096]{0,1:T(8,128)(2,1)} %bitcast.62) | data formatting | bytes 8388608 | tf_op jit(solution)/shard_map/dot_general | solution.py:134
  37.3 3.1 %collective-permute-start.3 = (bf16[256,1024]{1,0:T(8,128)(2,1)S(1)}, bf16[256,1024]{1,0:T(8,128)(2,1)S(1)}, u32[]{:S(2)}, u32[]{:S(2)}) collective-permute-start(bf16[256,1024]{1,0:T(8,128)(2,1)S(1)} %maximum_select_fusion.1), channel_id=1, source_target_pairs={{0,6},{1,7},{2,0},{3,1},{4,2},{5,3},{6,4},{7,5},{8,14},{9,15},{10,... | collective-permute-start | bytes 1572872 | tf_op jit(solution)/shard_map/ppermute | solution.py:97
  42.4 20.2 %collective-permute-done.3 = bf16[256,1024]{1,0:T(8,128)(2,1)S(1)} collective-permute-done((bf16[256,1024]{1,0:T(8,128)(2,1)S(1)}, bf16[256,1024]{1,0:T(8,128)(2,1)S(1)}, u32[]{:S(2)}, u32[]{:S(2)}) %collective-permute-start.3) | collective-permute-done | bytes 524320 | tf_op jit(solution)/shard_map/ppermute | solution.py:97
  62.6 3.7 %collective-permute-done.1 = bf16[256,1024]{1,0:T(8,128)(2,1)S(1)} collective-permute-done((bf16[256,1024]{1,0:T(8,128)(2,1)S(1)}, bf16[256,1024]{1,0:T(8,128)(2,1)S(1)}, u32[]{:S(2)}, u32[]{:S(2)}) %collective-permute-start.1) | collective-permute-done | bytes 524320 | tf_op jit(solution)/shard_map/ppermute | solution.py:97
  67.9 3.7 %gather_fusion = bf16[4,256,1024]{2,1,0:T(8,128)(2,1)} fusion(bf16[4,256,1024]{2,1,0:T(8,128)(2,1)} %pad_maximum_fusion, s32[1024]{0:T(1024)S(1)} %pad_clamp_fusion), kind=kCustom, calls=%fused_computation | custom fusion | bytes 4194320 | tf_op jit(solution)/shard_map/gather | solution.py:101
  77.0 4.0 %copy.43 = bf16[256,4,1024]{0,2,1:T(8,128)(2,1)} copy(bf16[256,4,1024]{2,0,1:T(8,128)(2,1)} %fusion.13) | data formatting | bytes 4194304 | tf_op jit(solution)/shard_map/convert_element_type | solution.py:21
  81.0 4.2 %fusion.45 = f32[256,2,2,128]{0,3,2,1:T(8,128)S(1)} fusion(bf16[256,4096,1,1]{0,1,3,2:T(8,128)(2,1)} %bitcast.64, bf16[2,2,128,4096]{3,2,1,0:T(8,128)(2,1)} %bitcast.68), kind=kOutput, calls=%fused_computation.91 | convolution fusion | flops 1073741824 | bytes 6815744 | tf_op jit(solution)/shard_map/dot_general | solution.py:134
  86.1 3.3 %collective-permute-start.4 = (bf16[2,256,2,128]{1,3,2,0:T(8,128)(2,1)S(1)}, bf16[2,256,2,128]{1,3,2,0:T(8,128)(2,1)S(1)}, u32[]{:S(2)}, u32[]{:S(2)}) collective-permute-start(bf16[2,256,2,128]{1,3,2,0:T(8,128)(2,1)S(1)} %pad_maximum_fusion.1), channel_id=1, source_target_pairs={{0,32},{8,40},{16,48},{24,56},{32,64},{40,72},{48,80},{56,88},{64,... | collective-permute-start | bytes 786440 | tf_op jit(solution)/shard_map/ppermute | solution.py:145
  91.6 3.9 %collective-permute-start.6 = (bf16[2,256,2,128]{1,3,2,0:T(8,128)(2,1)S(1)}, bf16[2,256,2,128]{1,3,2,0:T(8,128)(2,1)S(1)}, u32[]{:S(2)}, u32[]{:S(2)}) collective-permute-start(bf16[2,256,2,128]{1,3,2,0:T(8,128)(2,1)S(1)} %pad_maximum_fusion.1), channel_id=1, source_target_pairs={{0,16},{8,24},{16,32},{24,40},{32,48},{40,56},{48,64},{56,72},{64,... | collective-permute-start | bytes 786440 | tf_op jit(solution)/shard_map/ppermute | solution.py:145
  96.0 3.0 %collective-permute-start.7 = (bf16[2,256,2,128]{1,3,2,0:T(8,128)(2,1)S(1)}, bf16[2,256,2,128]{1,3,2,0:T(8,128)(2,1)S(1)}, u32[]{:S(2)}, u32[]{:S(2)}) collective-permute-start(bf16[2,256,2,128]{1,3,2,0:T(8,128)(2,1)S(1)} %pad_maximum_fusion.1), channel_id=1, source_target_pairs={{0,8},{8,16},{16,24},{24,32},{32,40},{40,48},{48,56},{56,64},{64,7... | collective-permute-start | bytes 786440 | tf_op jit(solution)/shard_map/ppermute | solution.py:145
  99.0 24.6 %collective-permute-done.4 = bf16[2,256,2,128]{1,3,2,0:T(8,128)(2,1)S(1)} collective-permute-done((bf16[2,256,2,128]{1,3,2,0:T(8,128)(2,1)S(1)}, bf16[2,256,2,128]{1,3,2,0:T(8,128)(2,1)S(1)}, u32[]{:S(2)}, u32[]{:S(2)}) %collective-permute-start.4) | collective-permute-done | bytes 262176 | tf_op jit(solution)/shard_map/ppermute | solution.py:145
  123.6 4.8 %collective-permute-done.5 = bf16[2,256,2,128]{1,3,2,0:T(8,128)(2,1)S(1)} collective-permute-done((bf16[2,256,2,128]{1,3,2,0:T(8,128)(2,1)S(1)}, bf16[2,256,2,128]{1,3,2,0:T(8,128)(2,1)S(1)}, u32[]{:S(2)}, u32[]{:S(2)}) %collective-permute-start.5) | collective-permute-done | bytes 262176 | tf_op jit(solution)/shard_map/ppermute | solution.py:145
  131.9 6.5 %select_reduce_fusion = (f32[2,256]{1,0:T(2,128)S(1)}, f32[2,256,8192]{2,1,0:T(8,128)S(1)}) fusion(pred[256,8192]{1,0:T(8,128)(4,1)} %broadcast_compare_fusion, bf16[8192,2,128]{0,2,1:T(8,128)(2,1)} %bitcast.78, bf16[256,2,96]{0,2,1:T(8,128)(2,1)S(1)} %slice.83, bf16[256,2,16]{0,2,1:T(8,128)(2,1)S(1)} %get-tuple-element.14, ...), kind=kOutput, calls=%fused_computation.2 | convolution fusion | flops 1086717440 | bytes 23201792 | tf_op jit(solution)/shard_map/qhd,khd->hqk/dot_general | solution.py:63
  138.4 5.7 %copy-done.2 = f32[2,256,8192]{2,1,0:T(8,128)} copy-done((f32[2,256,8192]{2,1,0:T(8,128)}, f32[2,256,8192]{2,1,0:T(8,128)S(1)}, u32[]{:S(2)}) %copy-start.2) | copy-done | bytes 16777240
  144.1 4.8 %fusion = f32[2,256]{1,0:T(2,128)S(1)} fusion(f32[2,256,8192]{2,1,0:T(8,128)S(1)} %get-tuple-element.19, f32[2,256]{1,0:T(2,128)S(1)} %max.7, pred[256,8192]{1,0:T(8,128)(4,1)S(1)} %copy-done.3), kind=kLoop, calls=%fused_computation.3 | loop fusion | flops 16776704 | bytes 18878464 | tf_op jit(solution)/shard_map/reduce_sum | solution.py:74
  148.9 13.7 %all-gather.5.cloned.1.call-done = bf16[8192,256]{1,0:T(8,128)(2,1)} async-done(((bf16[256,256]{1,0:T(8,128)(2,1)}), bf16[8192,256]{1,0:T(8,128)(2,1)}) %all-gather.5.cloned.1.call-update) | async-done | bytes 4194320 | tf_op jit(solution)/shard_map/all_gather | solution.py:120
  162.6 6.4 %copy.53 = bf16[8192,256]{0,1:T(8,128)(2,1)} copy(bf16[8192,256]{1,0:T(8,128)(2,1)} %all-gather.5.cloned.1.call-done) | data formatting | bytes 8388608 | tf_op jit(solution)/shard_map/all_gather | solution.py:120
  169.0 10.0 %fusion.2 = f32[2,256,128]{1,2,0:T(8,128)S(1)} fusion(bf16[8192,2,128]{0,2,1:T(8,128)(2,1)} %bitcast.69, f32[2,256,8192]{2,1,0:T(8,128)} %copy-done.2, f32[2,256]{1,0:T(2,128)S(1)} %max.7, pred[256,8192]{1,0:T(8,128)(4,1)} %broadcast_compare_fusion), kind=kOutput, calls=%fused_computation.5 | convolution fusion | flops 1090519040 | bytes 23332864 | tf_op jit(solution)/shard_map/hqk,khd->hqd/dot_general | solution.py:75
  181.7 60.2 %all_to_all.5 = bf16[8,32,4096]{2,1,0:T(8,128)(2,1)} all-to-all(bf16[8,32,4096]{2,1,0:T(8,128)(2,1)S(1)} %bitcast.66), channel_id=1, replica_groups=mesh['seq'=32,'mp'=8] {'mp'}, dimensions={0} | all-to-all | bytes 4194304 | tf_op jit(solution)/shard_map/all_to_all | solution.py:177
  242.0 2.7 %reduce_sum.92 = bf16[32,4096]{1,0:T(8,128)(2,1)} reduce(bf16[8,32,4096]{2,1,0:T(8,128)(2,1)} %all_to_all.5, bf16[]{:T(256)} %constant.90.clone.1), dimensions={0}, to_apply=%region_11.12 | reduce | flops 917504 | bytes 2359298 | tf_op jit(solution)/shard_map/reduce_sum | solution.py:180
  (84 shorter events, 23.9 us)
Async XLA Ops:
  6.5 174.4 %copy-start = (bf16[256,4096]{1,0:T(8,128)(2,1)S(1)}, bf16[256,4096]{1,0:T(8,128)(2,1)}, u32[]{:S(2)}) copy-start(bf16[256,4096]{1,0:T(8,128)(2,1)} %param.16) | copy-start | bytes 6291460
  6.5 15.1 %copy-start.10 = (bf16[4096]{0:T(1024)(128)(2,1)S(1)}, bf16[4096]{0:T(1024)(128)(2,1)}, u32[]{:S(2)}) copy-start(bf16[4096]{0:T(1024)(128)(2,1)} %param.13) | copy-start | bytes 24580
  6.5 15.1 %copy-start.11 = (bf16[4096]{0:T(1024)(128)(2,1)S(1)}, bf16[4096]{0:T(1024)(128)(2,1)}, u32[]{:S(2)}) copy-start(bf16[4096]{0:T(1024)(128)(2,1)} %param.12) | copy-start | bytes 24580
  6.5 125.4 %all-gather.3.cloned.1.call-start = ((), (), s32[]{:S(2)}) async-start(), calls=%async_computation.1 | async-start | bytes 4325376 | tf_op jit(solution)/shard_map/all_gather | solution.py:120
  8.4 154.2 %all-gather.5.cloned.1.call-start = ((), (), s32[]{:S(2)}) async-start(), calls=%async_computation.2 | async-start | bytes 4325376 | tf_op jit(solution)/shard_map/all_gather | solution.py:120
  8.4 28.8 %collective-permute-start = (bf16[256,512]{1,0:T(8,128)(2,1)}, bf16[256,512]{1,0:T(8,128)(2,1)S(1)}, u32[]{:S(2)}, u32[]{:S(2)}) collective-permute-start(bf16[256,512]{1,0:T(8,128)(2,1)} %param.11), channel_id=1, source_target_pairs={{0,1},{1,0},{2,3},{3,2},{4,5},{5,4},{6,7},{7,6},{8,9},{9,8},{10,11... | collective-permute-start | bytes 786440 | tf_op jit(solution)/shard_map/ppermute | solution.py:88
  30.7 6.5 %copy-start.7 = (bf16[256,512]{1,0:T(8,128)(2,1)S(1)}, bf16[256,512]{1,0:T(8,128)(2,1)}, u32[]{:S(2)}) copy-start(bf16[256,512]{1,0:T(8,128)(2,1)} %param.11) | copy-start | bytes 786436
  37.3 25.2 %collective-permute-start.3 = (bf16[256,1024]{1,0:T(8,128)(2,1)S(1)}, bf16[256,1024]{1,0:T(8,128)(2,1)S(1)}, u32[]{:S(2)}, u32[]{:S(2)}) collective-permute-start(bf16[256,1024]{1,0:T(8,128)(2,1)S(1)} %maximum_select_fusion.1), channel_id=1, source_target_pairs={{0,6},{1,7},{2,0},{3,1},{4,2},{5,3},{6,4},{7,5},{8,14},{9,15},{10,... | collective-permute-start | bytes 1572872 | tf_op jit(solution)/shard_map/ppermute | solution.py:97
  40.4 22.1 %collective-permute-start.2 = (bf16[256,1024]{1,0:T(8,128)(2,1)S(1)}, bf16[256,1024]{1,0:T(8,128)(2,1)S(1)}, u32[]{:S(2)}, u32[]{:S(2)}) collective-permute-start(bf16[256,1024]{1,0:T(8,128)(2,1)S(1)} %maximum_select_fusion.1), channel_id=1, source_target_pairs={{0,4},{1,5},{2,6},{3,7},{4,0},{5,1},{6,2},{7,3},{8,12},{9,13},{10,... | collective-permute-start | bytes 1572872 | tf_op jit(solution)/shard_map/ppermute | solution.py:97
  41.1 25.2 %collective-permute-start.1 = (bf16[256,1024]{1,0:T(8,128)(2,1)S(1)}, bf16[256,1024]{1,0:T(8,128)(2,1)S(1)}, u32[]{:S(2)}, u32[]{:S(2)}) collective-permute-start(bf16[256,1024]{1,0:T(8,128)(2,1)S(1)} %maximum_select_fusion.1), channel_id=1, source_target_pairs={{0,2},{1,3},{2,4},{3,5},{4,6},{5,7},{6,0},{7,1},{8,10},{9,11},{10,... | collective-permute-start | bytes 1572872 | tf_op jit(solution)/shard_map/ppermute | solution.py:97
  71.6 2.3 copy-start.1
  81.0 4.3 %copy-start.4 = (bf16[256,4096]{1,0:T(8,128)(2,1)S(1)}, bf16[256,4096]{1,0:T(8,128)(2,1)}, u32[]{:S(2)}) copy-start(bf16[256,4096]{1,0:T(8,128)(2,1)} %copy.61) | copy-start | bytes 6291460
  81.0 4.3 %copy-start.5 = (bf16[256,4,1024]{0,2,1:T(8,128)(2,1)S(1)}, bf16[256,4,1024]{0,2,1:T(8,128)(2,1)}, u32[]{:S(2)}) copy-start(bf16[256,4,1024]{0,2,1:T(8,128)(2,1)} %copy.43) | copy-start | bytes 6291460
  86.1 37.5 %collective-permute-start.4 = (bf16[2,256,2,128]{1,3,2,0:T(8,128)(2,1)S(1)}, bf16[2,256,2,128]{1,3,2,0:T(8,128)(2,1)S(1)}, u32[]{:S(2)}, u32[]{:S(2)}) collective-permute-start(bf16[2,256,2,128]{1,3,2,0:T(8,128)(2,1)S(1)} %pad_maximum_fusion.1), channel_id=1, source_target_pairs={{0,32},{8,40},{16,48},{24,56},{32,64},{40,72},{48,80},{56,88},{64,... | collective-permute-start | bytes 786440 | tf_op jit(solution)/shard_map/ppermute | solution.py:145
  89.4 39.0 %collective-permute-start.5 = (bf16[2,256,2,128]{1,3,2,0:T(8,128)(2,1)S(1)}, bf16[2,256,2,128]{1,3,2,0:T(8,128)(2,1)S(1)}, u32[]{:S(2)}, u32[]{:S(2)}) collective-permute-start(bf16[2,256,2,128]{1,3,2,0:T(8,128)(2,1)S(1)} %pad_maximum_fusion.1), channel_id=1, source_target_pairs={{0,24},{8,32},{16,40},{24,48},{32,56},{40,64},{48,72},{56,80},{64,... | collective-permute-start | bytes 786440 | tf_op jit(solution)/shard_map/ppermute | solution.py:145
  91.6 36.8 %collective-permute-start.6 = (bf16[2,256,2,128]{1,3,2,0:T(8,128)(2,1)S(1)}, bf16[2,256,2,128]{1,3,2,0:T(8,128)(2,1)S(1)}, u32[]{:S(2)}, u32[]{:S(2)}) collective-permute-start(bf16[2,256,2,128]{1,3,2,0:T(8,128)(2,1)S(1)} %pad_maximum_fusion.1), channel_id=1, source_target_pairs={{0,16},{8,24},{16,32},{24,40},{32,48},{40,56},{48,64},{56,72},{64,... | collective-permute-start | bytes 786440 | tf_op jit(solution)/shard_map/ppermute | solution.py:145
  96.0 32.5 %collective-permute-start.7 = (bf16[2,256,2,128]{1,3,2,0:T(8,128)(2,1)S(1)}, bf16[2,256,2,128]{1,3,2,0:T(8,128)(2,1)S(1)}, u32[]{:S(2)}, u32[]{:S(2)}) collective-permute-start(bf16[2,256,2,128]{1,3,2,0:T(8,128)(2,1)S(1)} %pad_maximum_fusion.1), channel_id=1, source_target_pairs={{0,8},{8,16},{16,24},{24,32},{32,40},{40,48},{48,56},{56,64},{64,7... | collective-permute-start | bytes 786440 | tf_op jit(solution)/shard_map/ppermute | solution.py:145
  128.5 1.1 copy-start.8
  131.9 12.2 %copy-start.3 = (pred[256,8192]{1,0:T(8,128)(4,1)S(1)}, pred[256,8192]{1,0:T(8,128)(4,1)}, u32[]{:S(2)}) copy-start(pred[256,8192]{1,0:T(8,128)(4,1)} %broadcast_compare_fusion) | copy-start | bytes 6291460
  138.4 5.7 %copy-start.2 = (f32[2,256,8192]{2,1,0:T(8,128)}, f32[2,256,8192]{2,1,0:T(8,128)S(1)}, u32[]{:S(2)}) copy-start(f32[2,256,8192]{2,1,0:T(8,128)S(1)} %get-tuple-element.19) | copy-start | bytes 50331652
  169.0 10.0 %copy-start.6 = (f32[2,256,1280]{2,1,0:T(8,128)S(1)}, f32[2,256,1280]{2,1,0:T(8,128)}, u32[]{:S(2)}) copy-start(f32[2,256,1280]{2,1,0:T(8,128)} %get-tuple-element.21) | copy-start | bytes 7864324
  178.9 1.3 copy-start.9
Sparse Core Ops, SparseCore 0:
  9.1 76.2 all-gather.2
  87.2 75.3 all-gather.4

commit v5 on v2

--- a/solution.py
+++ b/solution.py
@@ -174,10 +174,16 @@
     )
     partial = jnp.dot(heads_out, w_out, preferred_element_type=jnp.float32).astype(jnp.bfloat16)
     mp_count = lax.psum(1, "mp")
-    exchanged = lax.all_to_all(
-        partial.reshape(mp_count, token_count // mp_count, -1), "mp", 0, 0, tiled=False
-    )
-    return jnp.sum(exchanged.astype(jnp.float32), 0).astype(jnp.bfloat16)
+    mp_index = lax.axis_index("mp")
+    chunks = partial.reshape(mp_count, token_count // mp_count, -1)
+    total = chunks[mp_index].astype(jnp.float32)
+    for shift in range(1, mp_count):
+        outgoing = chunks[(mp_index + shift) % mp_count]
+        incoming = lax.ppermute(
+            outgoing, "mp", [(i, (i + shift) % mp_count) for i in range(mp_count)]
+        )
+        total = total + incoming.astype(jnp.float32)
+    return total.astype(jnp.bfloat16)
 
 
 def solution(mesh):

time: 227 us -> 224 us (0.987)
  blocking collectives: 55.9 us -> 0 us
  waiting for transfers between devices: 48.3 us -> 77.1 us
  starting transfers between devices: 24.3 us -> 45 us
  local copies, waits for them, and re-layouts: 34.8 us -> 39 us
    all_to_all x1 -> x0, blocking collectives: 55.9 us -> none  [body(): lax.all_to_all(partial.reshape(mp_count, token_count // mp_count, -1), 'm...]
    ppermute x0 -> x7, waiting for transfers between devices: none -> 29.6 us  [body(): lax.ppermute(outgoing, 'mp', [(i, (i + shift) % mp_count) for i in range(...]
    ppermute x0 -> x7, starting transfers between devices: none -> 20.7 us  [body(): lax.ppermute(outgoing, 'mp', [(i, (i + shift) % mp_count) for i in range(...]
    unnamed x31 -> x37, local copies, waits for them, and re-layouts: 9.83 us -> 13 us
    reduce_sum x1 -> x0, other arithmetic: 2.66 us -> none  [body(): return jnp.sum(exchanged.astype(jnp.float32), 0).astype(jnp.bfloat16)]
  transfers between devices with their start and end apart: 9 -> 16, of which waited for: 4 -> 9; matrix products, arithmetic and copies ran while one was open for 20% -> 21% of each run, Pallas kernels for 0% -> 0%
where the time goes in v5:
time: 224 us; the launch traced here: 221 us
  waiting for transfers between devices  77.1 us (34%)
  starting transfers between devices  45 us (20%)
  local copies, waits for them, and re-layouts  39 us (17%)
  matrix products  24.3 us (11%)
  other arithmetic  21.3 us (10%)
  between operations  13.9 us (6%)
    ppermute x7, waiting for transfers between devices, body(): lax.ppermute(outgoing, 'mp', [(i, (i + shift) % mp_count) for i in range(...  29.6 us
    ppermute x3, waiting for transfers between devices, gather_features(): lax.ppermute(pair, 'mp', [(i, (i + 2 * shift) % mp_count) for i in range(...  24 us
    ppermute x4, waiting for transfers between devices, body(): window.insert(0, lax.ppermute(key_value, 'seq', pairs))  23.5 us
    ppermute x7, starting transfers between devices, body(): lax.ppermute(outgoing, 'mp', [(i, (i + shift) % mp_count) for i in range(...  20.7 us
    unnamed x37, local copies, waits for them, and re-layouts  13 us
    ppermute x4, starting transfers between devices, body(): window.insert(0, lax.ppermute(key_value, 'seq', pairs))  12.3 us
    dot_general x2, matrix products, masked_softmax_attention(): jnp.einsum('hqk,khd->hqd', probs.astype(jnp.bfloat16), values, preferred_...  10.2 us
    dot_general x2, matrix products, masked_softmax_attention(): jnp.einsum('qhd,khd->hqk', queries, keys, preferred_element_type=jnp.floa...  8.37 us
  transfers between devices with their start and end apart: 16, of which 9 were waited for; matrix products, arithmetic and copies ran while one was open for 21% of the time, Pallas kernels for 0%

profile of v5, /device:TPU:2, one launch (start us, length us, event | category | flops | bytes accessed | tf_op | source)
XLA Modules:
  0.0 220.6 jit_solution(2154722100206253202)
XLA Ops:
  9.5 7.3 %collective-permute-start = (bf16[256,512]{1,0:T(8,128)(2,1)}, bf16[256,512]{1,0:T(8,128)(2,1)S(1)}, u32[]{:S(2)}, u32[]{:S(2)}) collective-permute-start(bf16[256,512]{1,0:T(8,128)(2,1)} %param.11), channel_id=1, source_target_pairs={{0,1},{1,0},{2,3},{3,2},{4,5},{5,4},{6,7},{7,6},{8,9},{9,8},{10,11... | collective-permute-start | bytes 786440 | tf_op jit(solution)/shard_map/ppermute | solution.py:88
  22.7 4.1 %copy.61 = bf16[256,4096]{1,0:T(8,128)(2,1)} copy(bf16[256,4096]{0,1:T(8,128)(2,1)} %bitcast.91) | data formatting | bytes 4194304 | tf_op jit(solution)/shard_map/dot_general | solution.py:131
  26.8 4.9 %copy.63 = bf16[512,8,2,256]{3,1,2,0:T(8,128)(2,1)} copy(bf16[512,8,2,256]{3,2,1,0:T(2,128)(2,1)} %bitcast.87) | data formatting | bytes 8388608
  31.6 6.4 %copy.50 = bf16[512,4096]{1,0:T(8,128)(2,1)} copy(bf16[512,4096]{0,1:T(8,128)(2,1)} %bitcast.81) | data formatting | bytes 8388608 | tf_op jit(solution)/shard_map/dot_general | solution.py:134
  38.2 3.1 %collective-permute-start.3 = (bf16[256,1024]{1,0:T(8,128)(2,1)S(1)}, bf16[256,1024]{1,0:T(8,128)(2,1)S(1)}, u32[]{:S(2)}, u32[]{:S(2)}) collective-permute-start(bf16[256,1024]{1,0:T(8,128)(2,1)S(1)} %maximum_select_fusion.1), channel_id=1, source_target_pairs={{0,6},{1,7},{2,0},{3,1},{4,2},{5,3},{6,4},{7,5},{8,14},{9,15},{10,... | collective-permute-start | bytes 1572872 | tf_op jit(solution)/shard_map/ppermute | solution.py:97
  43.2 20.3 %collective-permute-done.3 = bf16[256,1024]{1,0:T(8,128)(2,1)S(1)} collective-permute-done((bf16[256,1024]{1,0:T(8,128)(2,1)S(1)}, bf16[256,1024]{1,0:T(8,128)(2,1)S(1)}, u32[]{:S(2)}, u32[]{:S(2)}) %collective-permute-start.3) | collective-permute-done | bytes 524320 | tf_op jit(solution)/shard_map/ppermute | solution.py:97
  63.5 3.7 %collective-permute-done.1 = bf16[256,1024]{1,0:T(8,128)(2,1)S(1)} collective-permute-done((bf16[256,1024]{1,0:T(8,128)(2,1)S(1)}, bf16[256,1024]{1,0:T(8,128)(2,1)S(1)}, u32[]{:S(2)}, u32[]{:S(2)}) %collective-permute-start.1) | collective-permute-done | bytes 524320 | tf_op jit(solution)/shard_map/ppermute | solution.py:97
  68.8 3.6 %gather_fusion = bf16[4,256,1024]{2,1,0:T(8,128)(2,1)} fusion(bf16[4,256,1024]{2,1,0:T(8,128)(2,1)} %pad_maximum_fusion, s32[1024]{0:T(1024)S(1)} %pad_clamp_fusion), kind=kCustom, calls=%fused_computation | custom fusion | bytes 4194320 | tf_op jit(solution)/shard_map/gather | solution.py:101
  77.8 3.9 %copy.43 = bf16[256,4,1024]{0,2,1:T(8,128)(2,1)} copy(bf16[256,4,1024]{2,0,1:T(8,128)(2,1)} %fusion.13) | data formatting | bytes 4194304 | tf_op jit(solution)/shard_map/convert_element_type | solution.py:21
  81.8 4.4 %fusion.53 = f32[256,2,2,128]{0,3,2,1:T(8,128)S(1)} fusion(bf16[256,4096,1,1]{0,1,3,2:T(8,128)(2,1)} %bitcast.85, bf16[2,2,128,4096]{3,2,1,0:T(8,128)(2,1)} %bitcast.88), kind=kOutput, calls=%fused_computation.108 | convolution fusion | flops 1073741824 | bytes 6815744 | tf_op jit(solution)/shard_map/dot_general | solution.py:134
  87.0 3.3 %collective-permute-start.4 = (bf16[2,256,2,128]{1,3,2,0:T(8,128)(2,1)S(1)}, bf16[2,256,2,128]{1,3,2,0:T(8,128)(2,1)}, u32[]{:S(2)}, u32[]{:S(2)}) collective-permute-start(bf16[2,256,2,128]{1,3,2,0:T(8,128)(2,1)S(1)} %pad_maximum_fusion.2), channel_id=1, source_target_pairs={{0,32},{8,40},{16,48},{24,56},{32,64},{40,72},{48,80},{56,88},{64,... | collective-permute-start | bytes 786440 | tf_op jit(solution)/shard_map/ppermute | solution.py:145
  92.7 3.7 %collective-permute-start.6 = (bf16[2,256,2,128]{1,3,2,0:T(8,128)(2,1)S(1)}, bf16[2,256,2,128]{1,3,2,0:T(8,128)(2,1)S(1)}, u32[]{:S(2)}, u32[]{:S(2)}) collective-permute-start(bf16[2,256,2,128]{1,3,2,0:T(8,128)(2,1)S(1)} %pad_maximum_fusion.2), channel_id=1, source_target_pairs={{0,16},{8,24},{16,32},{24,40},{32,48},{40,56},{48,64},{56,72},{64,... | collective-permute-start | bytes 786440 | tf_op jit(solution)/shard_map/ppermute | solution.py:145
  96.9 3.0 %collective-permute-start.7 = (bf16[2,256,2,128]{1,3,2,0:T(8,128)(2,1)S(1)}, bf16[2,256,2,128]{1,3,2,0:T(8,128)(2,1)S(1)}, u32[]{:S(2)}, u32[]{:S(2)}) collective-permute-start(bf16[2,256,2,128]{1,3,2,0:T(8,128)(2,1)S(1)} %pad_maximum_fusion.2), channel_id=1, source_target_pairs={{0,8},{8,16},{16,24},{24,32},{32,40},{40,48},{48,56},{56,64},{64,7... | collective-permute-start | bytes 786440 | tf_op jit(solution)/shard_map/ppermute | solution.py:145
  99.9 22.0 %collective-permute-done.4 = bf16[2,256,2,128]{1,3,2,0:T(8,128)(2,1)} collective-permute-done((bf16[2,256,2,128]{1,3,2,0:T(8,128)(2,1)S(1)}, bf16[2,256,2,128]{1,3,2,0:T(8,128)(2,1)}, u32[]{:S(2)}, u32[]{:S(2)}) %collective-permute-start.4) | collective-permute-done | bytes 262176 | tf_op jit(solution)/shard_map/ppermute | solution.py:145
  128.8 6.1 %fusion.51 = (bf16[1,8192,256]{1,2,0:T(8,128)(2,1)}, bf16[1,8192,256]{1,2,0:T(8,128)(2,1)}) fusion(bf16[2,8192,256]{1,2,0:T(8,128)(2,1)} %all-gather.2.cloned.1.call-done), kind=kLoop, calls=%fused_computation.106 | loop fusion | bytes 16777216 | tf_op jit(solution)/shard_map/slice | solution.py:163
  134.9 6.1 %select_reduce_fusion = (f32[2,256]{1,0:T(2,128)S(1)}, f32[2,256,8192]{2,1,0:T(8,128)S(1)}) fusion(pred[256,8192]{1,0:T(8,128)(4,1)S(1)} %copy-done.3, bf16[8192,2,128]{0,2,1:T(8,128)(2,1)} %bitcast.90, bf16[256,2,96]{0,2,1:T(8,128)(2,1)S(1)} %copy-done.10, bf16[256,2,16]{0,2,1:T(8,128)(2,1)S(1)} %get-tuple-element.23, ...), kind=kOutput, calls=%fused_computation.2 | convolution fusion | flops 1086717440 | bytes 23201792 | tf_op jit(solution)/shard_map/qhd,khd->hqk/dot_general | solution.py:63
  141.0 4.8 %fusion = f32[2,256]{1,0:T(2,128)S(1)} fusion(f32[2,256,8192]{2,1,0:T(8,128)S(1)} %get-tuple-element.28, f32[2,256]{1,0:T(2,128)S(1)} %max.7, pred[256,8192]{1,0:T(8,128)(4,1)S(1)} %copy-done.3), kind=kLoop, calls=%fused_computation.3 | loop fusion | flops 16776704 | bytes 18878464 | tf_op jit(solution)/shard_map/reduce_sum | solution.py:74
  146.7 9.4 %fusion.2 = f32[2,256,128]{1,2,0:T(8,128)S(1)} fusion(bf16[8192,2,128]{0,2,1:T(8,128)(2,1)} %bitcast.89, f32[2,256,8192]{2,1,0:T(8,128)} %copy-done.2, f32[2,256]{1,0:T(2,128)S(1)} %max.7, pred[256,8192]{1,0:T(8,128)(4,1)S(1)} %copy-done.3), kind=kOutput, calls=%fused_computation.5 | convolution fusion | flops 1090519040 | bytes 23332864 | tf_op jit(solution)/shard_map/hqk,khd->hqd/dot_general | solution.py:75
  161.3 3.5 %collective-permute-start.14 = (bf16[32,4096]{1,0:T(8,128)(2,1)S(1)}, bf16[32,4096]{1,0:T(8,128)(2,1)S(1)}, u32[]{:S(2)}, u32[]{:S(2)}) collective-permute-start(bf16[32,4096]{1,0:T(8,128)(2,1)S(1)} %get-tuple-element.13), channel_id=1, source_target_pairs={{0,7},{1,0},{2,1},{3,2},{4,3},{5,4},{6,5},{7,6},{8,15},{9,8},{10,9... | collective-permute-start | bytes 786440 | tf_op jit(solution)/shard_map/ppermute | solution.py:182
  168.4 3.1 %collective-permute-start.11 = (bf16[32,4096]{1,0:T(8,128)(2,1)}, bf16[32,4096]{1,0:T(8,128)(2,1)S(1)}, u32[]{:S(2)}, u32[]{:S(2)}) collective-permute-start(bf16[32,4096]{1,0:T(8,128)(2,1)} %get-tuple-element.16), channel_id=1, source_target_pairs={{0,4},{1,5},{2,6},{3,7},{4,0},{5,1},{6,2},{7,3},{8,12},{9,13},{10,... | collective-permute-start | bytes 786440 | tf_op jit(solution)/shard_map/ppermute | solution.py:182
  172.7 16.0 %collective-permute-done.14 = bf16[32,4096]{1,0:T(8,128)(2,1)S(1)} collective-permute-done((bf16[32,4096]{1,0:T(8,128)(2,1)S(1)}, bf16[32,4096]{1,0:T(8,128)(2,1)S(1)}, u32[]{:S(2)}, u32[]{:S(2)}) %collective-permute-start.14) | collective-permute-done | bytes 262176 | tf_op jit(solution)/shard_map/ppermute | solution.py:182
  188.7 7.1 %collective-permute-start.9 = (bf16[32,4096]{1,0:T(8,128)(2,1)}, bf16[32,4096]{1,0:T(8,128)(2,1)}, u32[]{:S(2)}, u32[]{:S(2)}) collective-permute-start(bf16[32,4096]{1,0:T(8,128)(2,1)} %get-tuple-element.18), channel_id=1, source_target_pairs={{0,2},{1,3},{2,4},{3,5},{4,6},{5,7},{6,0},{7,1},{8,10},{9,11},{10,... | collective-permute-start | bytes 786440 | tf_op jit(solution)/shard_map/ppermute | solution.py:182
  200.9 4.1 %collective-permute-done.10 = bf16[32,4096]{1,0:T(8,128)(2,1)S(1)} collective-permute-done((bf16[32,4096]{1,0:T(8,128)(2,1)}, bf16[32,4096]{1,0:T(8,128)(2,1)S(1)}, u32[]{:S(2)}, u32[]{:S(2)}) %collective-permute-start.10) | collective-permute-done | bytes 262176 | tf_op jit(solution)/shard_map/ppermute | solution.py:182
  205.0 4.1 %collective-permute-done.9 = bf16[32,4096]{1,0:T(8,128)(2,1)} collective-permute-done((bf16[32,4096]{1,0:T(8,128)(2,1)}, bf16[32,4096]{1,0:T(8,128)(2,1)}, u32[]{:S(2)}, u32[]{:S(2)}) %collective-permute-start.9) | collective-permute-done | bytes 262176 | tf_op jit(solution)/shard_map/ppermute | solution.py:182
  (103 shorter events, 48.8 us)
Async XLA Ops:
  6.5 151.6 %copy-start = (bf16[256,4096]{1,0:T(8,128)(2,1)S(1)}, bf16[256,4096]{1,0:T(8,128)(2,1)}, u32[]{:S(2)}) copy-start(bf16[256,4096]{1,0:T(8,128)(2,1)} %param.16) | copy-start | bytes 6291460
  6.5 16.1 %copy-start.13 = (bf16[4096]{0:T(1024)(128)(2,1)S(1)}, bf16[4096]{0:T(1024)(128)(2,1)}, u32[]{:S(2)}) copy-start(bf16[4096]{0:T(1024)(128)(2,1)} %param.13) | copy-start | bytes 24580
  6.5 16.1 %copy-start.14 = (bf16[4096]{0:T(1024)(128)(2,1)S(1)}, bf16[4096]{0:T(1024)(128)(2,1)}, u32[]{:S(2)}) copy-start(bf16[4096]{0:T(1024)(128)(2,1)} %param.12) | copy-start | bytes 24580
  6.5 122.3 %all-gather.2.cloned.1.call-start = ((), (), s32[]{:S(2)}) async-start(), calls=%async_computation | async-start | bytes 8650752 | tf_op jit(solution)/shard_map/all_gather | solution.py:120
  9.5 28.6 %collective-permute-start = (bf16[256,512]{1,0:T(8,128)(2,1)}, bf16[256,512]{1,0:T(8,128)(2,1)S(1)}, u32[]{:S(2)}, u32[]{:S(2)}) collective-permute-start(bf16[256,512]{1,0:T(8,128)(2,1)} %param.11), channel_id=1, source_target_pairs={{0,1},{1,0},{2,3},{3,2},{4,5},{5,4},{6,7},{7,6},{8,9},{9,8},{10,11... | collective-permute-start | bytes 786440 | tf_op jit(solution)/shard_map/ppermute | solution.py:88
  31.6 6.4 %copy-start.8 = (bf16[256,512]{1,0:T(8,128)(2,1)S(1)}, bf16[256,512]{1,0:T(8,128)(2,1)}, u32[]{:S(2)}) copy-start(bf16[256,512]{1,0:T(8,128)(2,1)} %param.11) | copy-start | bytes 786436
  38.2 25.3 %collective-permute-start.3 = (bf16[256,1024]{1,0:T(8,128)(2,1)S(1)}, bf16[256,1024]{1,0:T(8,128)(2,1)S(1)}, u32[]{:S(2)}, u32[]{:S(2)}) collective-permute-start(bf16[256,1024]{1,0:T(8,128)(2,1)S(1)} %maximum_select_fusion.1), channel_id=1, source_target_pairs={{0,6},{1,7},{2,0},{3,1},{4,2},{5,3},{6,4},{7,5},{8,14},{9,15},{10,... | collective-permute-start | bytes 1572872 | tf_op jit(solution)/shard_map/ppermute | solution.py:97
  41.3 22.2 %collective-permute-start.2 = (bf16[256,1024]{1,0:T(8,128)(2,1)S(1)}, bf16[256,1024]{1,0:T(8,128)(2,1)S(1)}, u32[]{:S(2)}, u32[]{:S(2)}) collective-permute-start(bf16[256,1024]{1,0:T(8,128)(2,1)S(1)} %maximum_select_fusion.1), channel_id=1, source_target_pairs={{0,4},{1,5},{2,6},{3,7},{4,0},{5,1},{6,2},{7,3},{8,12},{9,13},{10,... | collective-permute-start | bytes 1572872 | tf_op jit(solution)/shard_map/ppermute | solution.py:97
  42.0 25.2 %collective-permute-start.1 = (bf16[256,1024]{1,0:T(8,128)(2,1)S(1)}, bf16[256,1024]{1,0:T(8,128)(2,1)S(1)}, u32[]{:S(2)}, u32[]{:S(2)}) collective-permute-start(bf16[256,1024]{1,0:T(8,128)(2,1)S(1)} %maximum_select_fusion.1), channel_id=1, source_target_pairs={{0,2},{1,3},{2,4},{3,5},{4,6},{5,7},{6,0},{7,1},{8,10},{9,11},{10,... | collective-permute-start | bytes 1572872 | tf_op jit(solution)/shard_map/ppermute | solution.py:97
  87.0 34.9 %collective-permute-start.4 = (bf16[2,256,2,128]{1,3,2,0:T(8,128)(2,1)S(1)}, bf16[2,256,2,128]{1,3,2,0:T(8,128)(2,1)}, u32[]{:S(2)}, u32[]{:S(2)}) collective-permute-start(bf16[2,256,2,128]{1,3,2,0:T(8,128)(2,1)S(1)} %pad_maximum_fusion.2), channel_id=1, source_target_pairs={{0,32},{8,40},{16,48},{24,56},{32,64},{40,72},{48,80},{56,88},{64,... | collective-permute-start | bytes 786440 | tf_op jit(solution)/shard_map/ppermute | solution.py:145
  90.4 34.0 %collective-permute-start.5 = (bf16[2,256,2,128]{1,3,2,0:T(8,128)(2,1)S(1)}, bf16[2,256,2,128]{1,3,2,0:T(8,128)(2,1)}, u32[]{:S(2)}, u32[]{:S(2)}) collective-permute-start(bf16[2,256,2,128]{1,3,2,0:T(8,128)(2,1)S(1)} %pad_maximum_fusion.2), channel_id=1, source_target_pairs={{0,24},{8,32},{16,40},{24,48},{32,56},{40,64},{48,72},{56,80},{64,... | collective-permute-start | bytes 786440 | tf_op jit(solution)/shard_map/ppermute | solution.py:145
  92.7 32.6 %collective-permute-start.6 = (bf16[2,256,2,128]{1,3,2,0:T(8,128)(2,1)S(1)}, bf16[2,256,2,128]{1,3,2,0:T(8,128)(2,1)S(1)}, u32[]{:S(2)}, u32[]{:S(2)}) collective-permute-start(bf16[2,256,2,128]{1,3,2,0:T(8,128)(2,1)S(1)} %pad_maximum_fusion.2), channel_id=1, source_target_pairs={{0,16},{8,24},{16,32},{24,40},{32,48},{40,56},{48,64},{56,72},{64,... | collective-permute-start | bytes 786440 | tf_op jit(solution)/shard_map/ppermute | solution.py:145
  96.9 28.5 %copy-start.9 = (bf16[256,2,96]{0,2,1:T(8,128)(2,1)}, bf16[256,2,96]{0,2,1:T(8,128)(2,1)S(1)}, u32[]{:S(2)}) copy-start(bf16[256,2,96]{0,2,1:T(8,128)(2,1)S(1)} %slice.93) | copy-start | bytes 294916
  96.9 28.5 %collective-permute-start.7 = (bf16[2,256,2,128]{1,3,2,0:T(8,128)(2,1)S(1)}, bf16[2,256,2,128]{1,3,2,0:T(8,128)(2,1)S(1)}, u32[]{:S(2)}, u32[]{:S(2)}) collective-permute-start(bf16[2,256,2,128]{1,3,2,0:T(8,128)(2,1)S(1)} %pad_maximum_fusion.2), channel_id=1, source_target_pairs={{0,8},{8,16},{16,24},{24,32},{32,40},{40,48},{48,56},{56,64},{64,7... | collective-permute-start | bytes 786440 | tf_op jit(solution)/shard_map/ppermute | solution.py:145
  128.8 6.1 %copy-start.10 = (bf16[256,2,96]{0,2,1:T(8,128)(2,1)S(1)}, bf16[256,2,96]{0,2,1:T(8,128)(2,1)}, u32[]{:S(2)}) copy-start(bf16[256,2,96]{0,2,1:T(8,128)(2,1)} %copy-done.9) | copy-start | bytes 294916
  128.8 6.1 %copy-start.3 = (pred[256,8192]{1,0:T(8,128)(4,1)S(1)}, pred[256,8192]{1,0:T(8,128)(4,1)}, u32[]{:S(2)}) copy-start(pred[256,8192]{1,0:T(8,128)(4,1)} %broadcast_compare_fusion) | copy-start | bytes 6291460
  146.7 9.5 %copy-start.7 = (f32[2,256,1280]{2,1,0:T(8,128)S(1)}, f32[2,256,1280]{2,1,0:T(8,128)}, u32[]{:S(2)}) copy-start(f32[2,256,1280]{2,1,0:T(8,128)} %get-tuple-element.30) | copy-start | bytes 7864324
  161.3 27.4 %collective-permute-start.14 = (bf16[32,4096]{1,0:T(8,128)(2,1)S(1)}, bf16[32,4096]{1,0:T(8,128)(2,1)S(1)}, u32[]{:S(2)}, u32[]{:S(2)}) collective-permute-start(bf16[32,4096]{1,0:T(8,128)(2,1)S(1)} %get-tuple-element.13), channel_id=1, source_target_pairs={{0,7},{1,0},{2,1},{3,2},{4,3},{5,4},{6,5},{7,6},{8,15},{9,8},{10,9... | collective-permute-start | bytes 786440 | tf_op jit(solution)/shard_map/ppermute | solution.py:182
  164.8 31.0 %collective-permute-start.13 = (bf16[32,4096]{1,0:T(8,128)(2,1)S(1)}, bf16[32,4096]{1,0:T(8,128)(2,1)S(1)}, u32[]{:S(2)}, u32[]{:S(2)}) collective-permute-start(bf16[32,4096]{1,0:T(8,128)(2,1)S(1)} %get-tuple-element.14), channel_id=1, source_target_pairs={{0,6},{1,7},{2,0},{3,1},{4,2},{5,3},{6,4},{7,5},{8,14},{9,15},{10,... | collective-permute-start | bytes 786440 | tf_op jit(solution)/shard_map/ppermute | solution.py:182
  165.4 35.5 %collective-permute-start.12 = (bf16[32,4096]{1,0:T(8,128)(2,1)}, bf16[32,4096]{1,0:T(8,128)(2,1)S(1)}, u32[]{:S(2)}, u32[]{:S(2)}) collective-permute-start(bf16[32,4096]{1,0:T(8,128)(2,1)} %get-tuple-element.15), channel_id=1, source_target_pairs={{0,5},{1,6},{2,7},{3,0},{4,1},{5,2},{6,3},{7,4},{8,13},{9,14},{10,... | collective-permute-start | bytes 786440 | tf_op jit(solution)/shard_map/ppermute | solution.py:182
  168.4 32.5 %collective-permute-start.11 = (bf16[32,4096]{1,0:T(8,128)(2,1)}, bf16[32,4096]{1,0:T(8,128)(2,1)S(1)}, u32[]{:S(2)}, u32[]{:S(2)}) collective-permute-start(bf16[32,4096]{1,0:T(8,128)(2,1)} %get-tuple-element.16), channel_id=1, source_target_pairs={{0,4},{1,5},{2,6},{3,7},{4,0},{5,1},{6,2},{7,3},{8,12},{9,13},{10,... | collective-permute-start | bytes 786440 | tf_op jit(solution)/shard_map/ppermute | solution.py:182
  171.5 33.5 %collective-permute-start.10 = (bf16[32,4096]{1,0:T(8,128)(2,1)}, bf16[32,4096]{1,0:T(8,128)(2,1)S(1)}, u32[]{:S(2)}, u32[]{:S(2)}) collective-permute-start(bf16[32,4096]{1,0:T(8,128)(2,1)} %get-tuple-element.17), channel_id=1, source_target_pairs={{0,3},{1,4},{2,5},{3,6},{4,7},{5,0},{6,1},{7,2},{8,11},{9,12},{10,... | collective-permute-start | bytes 786440 | tf_op jit(solution)/shard_map/ppermute | solution.py:182
  188.7 20.3 %collective-permute-start.9 = (bf16[32,4096]{1,0:T(8,128)(2,1)}, bf16[32,4096]{1,0:T(8,128)(2,1)}, u32[]{:S(2)}, u32[]{:S(2)}) collective-permute-start(bf16[32,4096]{1,0:T(8,128)(2,1)} %get-tuple-element.18), channel_id=1, source_target_pairs={{0,2},{1,3},{2,4},{3,5},{4,6},{5,7},{6,0},{7,1},{8,10},{9,11},{10,... | collective-permute-start | bytes 786440 | tf_op jit(solution)/shard_map/ppermute | solution.py:182
  195.8 15.8 %collective-permute-start.8 = (bf16[32,4096]{1,0:T(8,128)(2,1)}, bf16[32,4096]{1,0:T(8,128)(2,1)}, u32[]{:S(2)}, u32[]{:S(2)}) collective-permute-start(bf16[32,4096]{1,0:T(8,128)(2,1)} %get-tuple-element.12), channel_id=1, source_target_pairs={{0,1},{1,2},{2,3},{3,4},{4,5},{5,6},{6,7},{7,0},{8,9},{9,10},{10,1... | collective-permute-start | bytes 786440 | tf_op jit(solution)/shard_map/ppermute | solution.py:182
  (7 other events, 20.7 us)
Sparse Core Ops, SparseCore 0:
  9.6 94.1 all-gather.1

commit v6 on v5

--- a/solution.py
+++ b/solution.py
@@ -175,14 +175,20 @@
     partial = jnp.dot(heads_out, w_out, preferred_element_type=jnp.float32).astype(jnp.bfloat16)
     mp_count = lax.psum(1, "mp")
     mp_index = lax.axis_index("mp")
-    chunks = partial.reshape(mp_count, token_count // mp_count, -1)
-    total = chunks[mp_index].astype(jnp.float32)
-    for shift in range(1, mp_count):
-        outgoing = chunks[(mp_index + shift) % mp_count]
+    ring = mp_count // 2
+    ring_index = mp_index // 2
+    chunks = partial.reshape(ring, token_count // ring, -1)
+    ring_total = chunks[ring_index].astype(jnp.float32)
+    for shift in range(1, ring):
+        outgoing = chunks[(ring_index + shift) % ring]
         incoming = lax.ppermute(
-            outgoing, "mp", [(i, (i + shift) % mp_count) for i in range(mp_count)]
+            outgoing, "mp", [(i, (i + 2 * shift) % mp_count) for i in range(mp_count)]
         )
-        total = total + incoming.astype(jnp.float32)
+        ring_total = ring_total + incoming.astype(jnp.float32)
+    halves = ring_total.reshape(2, token_count // mp_count, -1)
+    side = mp_index % 2
+    swapped = lax.ppermute(halves[1 - side], "mp", [(i, i ^ 1) for i in range(mp_count)])
+    total = halves[side] + swapped
     return total.astype(jnp.bfloat16)
 
 

time: 224 us -> 229 us (1.022)
  waiting for transfers between devices: 77.1 us -> 94.8 us
  starting transfers between devices: 45 us -> 31.7 us
    ppermute x7 -> x4, waiting for transfers between devices: 29.6 us -> 47.4 us  [the longest x1 24.1 us: body(): lax.ppermute(halves[1 - side], 'mp', [(i, i ^ 1) for i in range(mp_count)])]
    ppermute x7 -> x4, starting transfers between devices: 20.7 us -> 7.37 us  [the longest x1 4.23 us: body(): lax.ppermute(halves[1 - side], 'mp', [(i, i ^ 1) for i in range(mp_count)])]
  transfers between devices with their start and end apart: 16 -> 13, of which waited for: 9 -> 7; matrix products, arithmetic and copies ran while one was open for 21% -> 20% of each run, Pallas kernels for 0% -> 0%
where the time goes in v6:
time: 229 us; the launch traced here: 227 us
  waiting for transfers between devices  94.8 us (41%)
  local copies, waits for them, and re-layouts  39.8 us (17%)
  starting transfers between devices  31.7 us (14%)
  matrix products  24.3 us (11%)
  other arithmetic  22.7 us (10%)
  between operations  13.9 us (6%)
    ppermute x1, waiting for transfers between devices, body(): lax.ppermute(halves[1 - side], 'mp', [(i, i ^ 1) for i in range(mp_count)])  24.1 us
    ppermute x3, waiting for transfers between devices, gather_features(): lax.ppermute(pair, 'mp', [(i, (i + 2 * shift) % mp_count) for i in range(...  24 us
    ppermute x4, waiting for transfers between devices, body(): window.insert(0, lax.ppermute(key_value, 'seq', pairs))  23.4 us
    ppermute x3, waiting for transfers between devices, body(): lax.ppermute(outgoing, 'mp', [(i, (i + 2 * shift) % mp_count) for i in ra...  23.3 us
    unnamed x37, local copies, waits for them, and re-layouts  13 us
    ppermute x4, starting transfers between devices, body(): window.insert(0, lax.ppermute(key_value, 'seq', pairs))  12.3 us
    dot_general x2, matrix products, masked_softmax_attention(): jnp.einsum('hqk,khd->hqd', probs.astype(jnp.bfloat16), values, preferred_...  10.2 us
    dot_general x2, matrix products, masked_softmax_attention(): jnp.einsum('qhd,khd->hqk', queries, keys, preferred_element_type=jnp.floa...  8.37 us
  transfers between devices with their start and end apart: 13, of which 7 were waited for; matrix products, arithmetic and copies ran while one was open for 20% of the time, Pallas kernels for 0%

profile of v6, /device:TPU:2, one launch (start us, length us, event | category | flops | bytes accessed | tf_op | source)
XLA Modules:
  0.0 227.2 jit_solution(16513660681882025384)
XLA Ops:
  9.5 7.3 %collective-permute-start = (bf16[256,512]{1,0:T(8,128)(2,1)}, bf16[256,512]{1,0:T(8,128)(2,1)S(1)}, u32[]{:S(2)}, u32[]{:S(2)}) collective-permute-start(bf16[256,512]{1,0:T(8,128)(2,1)} %param.11), channel_id=1, source_target_pairs={{0,1},{1,0},{2,3},{3,2},{4,5},{5,4},{6,7},{7,6},{8,9},{9,8},{10,11... | collective-permute-start | bytes 786440 | tf_op jit(solution)/shard_map/ppermute | solution.py:88
  20.0 2.6 %broadcast_compare_fusion = pred[256,8192]{1,0:T(8,128)(4,1)} fusion(s32[8192]{0:T(1024)S(1)} %add_bitcast_fusion, s32[256]{0:T(256)S(1)} %get-tuple-element.7), kind=kLoop, calls=%fused_computation.16 | loop fusion | flops 2097152 | bytes 2130944 | tf_op jit(solution)/shard_map/lt | solution.py:162
  22.7 4.1 %copy.61 = bf16[256,4096]{1,0:T(8,128)(2,1)} copy(bf16[256,4096]{0,1:T(8,128)(2,1)} %bitcast.92) | data formatting | bytes 4194304 | tf_op jit(solution)/shard_map/dot_general | solution.py:131
  26.8 4.9 %copy.63 = bf16[512,8,2,256]{3,1,2,0:T(8,128)(2,1)} copy(bf16[512,8,2,256]{3,2,1,0:T(2,128)(2,1)} %bitcast.86) | data formatting | bytes 8388608
  31.7 6.4 %copy.50 = bf16[512,4096]{1,0:T(8,128)(2,1)} copy(bf16[512,4096]{0,1:T(8,128)(2,1)} %bitcast.80) | data formatting | bytes 8388608 | tf_op jit(solution)/shard_map/dot_general | solution.py:134
  38.3 3.1 %collective-permute-start.3 = (bf16[256,1024]{1,0:T(8,128)(2,1)S(1)}, bf16[256,1024]{1,0:T(8,128)(2,1)S(1)}, u32[]{:S(2)}, u32[]{:S(2)}) collective-permute-start(bf16[256,1024]{1,0:T(8,128)(2,1)S(1)} %maximum_select_fusion.1), channel_id=1, source_target_pairs={{0,6},{1,7},{2,0},{3,1},{4,2},{5,3},{6,4},{7,5},{8,14},{9,15},{10,... | collective-permute-start | bytes 1572872 | tf_op jit(solution)/shard_map/ppermute | solution.py:97
  43.3 20.3 %collective-permute-done.3 = bf16[256,1024]{1,0:T(8,128)(2,1)S(1)} collective-permute-done((bf16[256,1024]{1,0:T(8,128)(2,1)S(1)}, bf16[256,1024]{1,0:T(8,128)(2,1)S(1)}, u32[]{:S(2)}, u32[]{:S(2)}) %collective-permute-start.3) | collective-permute-done | bytes 524320 | tf_op jit(solution)/shard_map/ppermute | solution.py:97
  63.5 3.7 %collective-permute-done.1 = bf16[256,1024]{1,0:T(8,128)(2,1)S(1)} collective-permute-done((bf16[256,1024]{1,0:T(8,128)(2,1)S(1)}, bf16[256,1024]{1,0:T(8,128)(2,1)S(1)}, u32[]{:S(2)}, u32[]{:S(2)}) %collective-permute-start.1) | collective-permute-done | bytes 524320 | tf_op jit(solution)/shard_map/ppermute | solution.py:97
  68.8 3.6 %gather_fusion = bf16[4,256,1024]{2,1,0:T(8,128)(2,1)} fusion(bf16[4,256,1024]{2,1,0:T(8,128)(2,1)} %pad_maximum_fusion, s32[1024]{0:T(1024)S(1)} %pad_clamp_fusion), kind=kCustom, calls=%fused_computation | custom fusion | bytes 4194320 | tf_op jit(solution)/shard_map/gather | solution.py:101
  75.5 2.4 %fusion.13 = bf16[256,4,1024]{2,0,1:T(8,128)(2,1)} fusion(bf16[4,256,1024]{2,1,0:T(8,128)(2,1)S(1)} %copy-done.1, f32[4,1024]{1,0:T(4,128)S(1)} %reshape.480, f32[4,1024]{1,0:T(4,128)S(1)} %reshape.479, f32[256]{0:T(256)S(1)} %add_rsqrt_fusion, f32[256]{0:T(256)S(1)} %broadcast_multiply_fusion), kind=kLoop, calls=%fused_computation.22 | loop fusion | flops 6291456 | bytes 4229120 | tf_op jit(solution)/shard_map/convert_element_type | solution.py:21
  77.9 3.9 %copy.43 = bf16[256,4,1024]{0,2,1:T(8,128)(2,1)} copy(bf16[256,4,1024]{2,0,1:T(8,128)(2,1)} %fusion.13) | data formatting | bytes 4194304 | tf_op jit(solution)/shard_map/convert_element_type | solution.py:21
  81.8 4.4 %fusion.49 = f32[256,2,2,128]{0,3,2,1:T(8,128)S(1)} fusion(bf16[256,4096,1,1]{0,1,3,2:T(8,128)(2,1)} %bitcast.84, bf16[2,2,128,4096]{3,2,1,0:T(8,128)(2,1)} %bitcast.87), kind=kOutput, calls=%fused_computation.102 | convolution fusion | flops 1073741824 | bytes 6815744 | tf_op jit(solution)/shard_map/dot_general | solution.py:134
  87.1 3.4 %collective-permute-start.4 = (bf16[2,256,2,128]{1,3,2,0:T(8,128)(2,1)S(1)}, bf16[2,256,2,128]{1,3,2,0:T(8,128)(2,1)}, u32[]{:S(2)}, u32[]{:S(2)}) collective-permute-start(bf16[2,256,2,128]{1,3,2,0:T(8,128)(2,1)S(1)} %pad_maximum_fusion.2), channel_id=1, source_target_pairs={{0,32},{8,40},{16,48},{24,56},{32,64},{40,72},{48,80},{56,88},{64,... | collective-permute-start | bytes 786440 | tf_op jit(solution)/shard_map/ppermute | solution.py:145
  92.7 3.7 %collective-permute-start.6 = (bf16[2,256,2,128]{1,3,2,0:T(8,128)(2,1)S(1)}, bf16[2,256,2,128]{1,3,2,0:T(8,128)(2,1)S(1)}, u32[]{:S(2)}, u32[]{:S(2)}) collective-permute-start(bf16[2,256,2,128]{1,3,2,0:T(8,128)(2,1)S(1)} %pad_maximum_fusion.2), channel_id=1, source_target_pairs={{0,16},{8,24},{16,32},{24,40},{32,48},{40,56},{48,64},{56,72},{64,... | collective-permute-start | bytes 786440 | tf_op jit(solution)/shard_map/ppermute | solution.py:145
  97.0 3.0 %collective-permute-start.7 = (bf16[2,256,2,128]{1,3,2,0:T(8,128)(2,1)S(1)}, bf16[2,256,2,128]{1,3,2,0:T(8,128)(2,1)S(1)}, u32[]{:S(2)}, u32[]{:S(2)}) collective-permute-start(bf16[2,256,2,128]{1,3,2,0:T(8,128)(2,1)S(1)} %pad_maximum_fusion.2), channel_id=1, source_target_pairs={{0,8},{8,16},{16,24},{24,32},{32,40},{40,48},{48,56},{56,64},{64,7... | collective-permute-start | bytes 786440 | tf_op jit(solution)/shard_map/ppermute | solution.py:145
  99.9 22.0 %collective-permute-done.4 = bf16[2,256,2,128]{1,3,2,0:T(8,128)(2,1)} collective-permute-done((bf16[2,256,2,128]{1,3,2,0:T(8,128)(2,1)S(1)}, bf16[2,256,2,128]{1,3,2,0:T(8,128)(2,1)}, u32[]{:S(2)}, u32[]{:S(2)}) %collective-permute-start.4) | collective-permute-done | bytes 262176 | tf_op jit(solution)/shard_map/ppermute | solution.py:145
  128.8 6.0 %fusion.47 = (bf16[1,8192,256]{1,2,0:T(8,128)(2,1)}, bf16[1,8192,256]{1,2,0:T(8,128)(2,1)}) fusion(bf16[2,8192,256]{1,2,0:T(8,128)(2,1)} %all-gather.2.cloned.1.call-done), kind=kLoop, calls=%fused_computation.100 | loop fusion | bytes 16777216 | tf_op jit(solution)/shard_map/slice | solution.py:163
  134.8 6.1 %select_reduce_fusion = (f32[2,256]{1,0:T(2,128)S(1)}, f32[2,256,8192]{2,1,0:T(8,128)S(1)}) fusion(pred[256,8192]{1,0:T(8,128)(4,1)S(1)} %copy-done.3, bf16[8192,2,128]{0,2,1:T(8,128)(2,1)} %bitcast.91, bf16[256,2,96]{0,2,1:T(8,128)(2,1)S(1)} %copy-done.10, bf16[256,2,16]{0,2,1:T(8,128)(2,1)S(1)} %get-tuple-element.19, ...), kind=kOutput, calls=%fused_computation.2 | convolution fusion | flops 1086717440 | bytes 23201792 | tf_op jit(solution)/shard_map/qhd,khd->hqk/dot_general | solution.py:63
  140.9 4.8 %fusion = f32[2,256]{1,0:T(2,128)S(1)} fusion(f32[2,256,8192]{2,1,0:T(8,128)S(1)} %get-tuple-element.24, f32[2,256]{1,0:T(2,128)S(1)} %max.7, pred[256,8192]{1,0:T(8,128)(4,1)S(1)} %copy-done.3), kind=kLoop, calls=%fused_computation.3 | loop fusion | flops 16776704 | bytes 18878464 | tf_op jit(solution)/shard_map/reduce_sum | solution.py:74
  146.6 9.4 %fusion.2 = f32[2,256,128]{1,2,0:T(8,128)S(1)} fusion(bf16[8192,2,128]{0,2,1:T(8,128)(2,1)} %bitcast.90, f32[2,256,8192]{2,1,0:T(8,128)} %copy-done.2, f32[2,256]{1,0:T(2,128)S(1)} %max.7, pred[256,8192]{1,0:T(8,128)(4,1)S(1)} %copy-done.3), kind=kOutput, calls=%fused_computation.5 | convolution fusion | flops 1090519040 | bytes 23332864 | tf_op jit(solution)/shard_map/hqk,khd->hqd/dot_general | solution.py:75
  164.3 19.9 %collective-permute-done.10 = bf16[64,4096]{1,0:T(8,128)(2,1)} collective-permute-done((bf16[64,4096]{1,0:T(8,128)(2,1)}, bf16[64,4096]{1,0:T(8,128)(2,1)}, u32[]{:S(2)}, u32[]{:S(2)}) %collective-permute-start.10) | collective-permute-done | bytes 524320 | tf_op jit(solution)/shard_map/ppermute | solution.py:184
  184.2 3.4 %collective-permute-done.8 = bf16[64,4096]{1,0:T(8,128)(2,1)} collective-permute-done((bf16[64,4096]{1,0:T(8,128)(2,1)S(1)}, bf16[64,4096]{1,0:T(8,128)(2,1)}, u32[]{:S(2)}, u32[]{:S(2)}) %collective-permute-start.8) | collective-permute-done | bytes 524320 | tf_op jit(solution)/shard_map/ppermute | solution.py:184
  190.2 4.2 %collective-permute-start.11 = (f32[32,4096]{1,0:T(8,128)}, f32[32,4096]{1,0:T(8,128)}, u32[]{:S(2)}, u32[]{:S(2)}) collective-permute-start(f32[32,4096]{1,0:T(8,128)} %dynamic-slice_bitcast_fusion), channel_id=1, source_target_pairs={{0,1},{1,0},{2,3},{3,2},{4,5},{5,4},{6,7},{7,6},{8,9},{9,8},{10,11... | collective-permute-start | bytes 1572872 | tf_op jit(solution)/shard_map/ppermute | solution.py:190
  194.5 24.1 %collective-permute-done.11 = f32[32,4096]{1,0:T(8,128)} collective-permute-done((f32[32,4096]{1,0:T(8,128)}, f32[32,4096]{1,0:T(8,128)}, u32[]{:S(2)}, u32[]{:S(2)}) %collective-permute-start.11) | collective-permute-done | bytes 524320 | tf_op jit(solution)/shard_map/ppermute | solution.py:190
  (99 shorter events, 36.6 us)
Async XLA Ops:
  6.5 151.6 %copy-start = (bf16[256,4096]{1,0:T(8,128)(2,1)S(1)}, bf16[256,4096]{1,0:T(8,128)(2,1)}, u32[]{:S(2)}) copy-start(bf16[256,4096]{1,0:T(8,128)(2,1)} %param.16) | copy-start | bytes 6291460
  6.5 16.1 %copy-start.13 = (bf16[4096]{0:T(1024)(128)(2,1)S(1)}, bf16[4096]{0:T(1024)(128)(2,1)}, u32[]{:S(2)}) copy-start(bf16[4096]{0:T(1024)(128)(2,1)} %param.13) | copy-start | bytes 24580
  6.5 16.1 %copy-start.14 = (bf16[4096]{0:T(1024)(128)(2,1)S(1)}, bf16[4096]{0:T(1024)(128)(2,1)}, u32[]{:S(2)}) copy-start(bf16[4096]{0:T(1024)(128)(2,1)} %param.12) | copy-start | bytes 24580
  6.5 122.2 %all-gather.2.cloned.1.call-start = ((), (), s32[]{:S(2)}) async-start(), calls=%async_computation | async-start | bytes 8650752 | tf_op jit(solution)/shard_map/all_gather | solution.py:120
  9.5 28.7 %collective-permute-start = (bf16[256,512]{1,0:T(8,128)(2,1)}, bf16[256,512]{1,0:T(8,128)(2,1)S(1)}, u32[]{:S(2)}, u32[]{:S(2)}) collective-permute-start(bf16[256,512]{1,0:T(8,128)(2,1)} %param.11), channel_id=1, source_target_pairs={{0,1},{1,0},{2,3},{3,2},{4,5},{5,4},{6,7},{7,6},{8,9},{9,8},{10,11... | collective-permute-start | bytes 786440 | tf_op jit(solution)/shard_map/ppermute | solution.py:88
  31.7 6.4 %copy-start.8 = (bf16[256,512]{1,0:T(8,128)(2,1)S(1)}, bf16[256,512]{1,0:T(8,128)(2,1)}, u32[]{:S(2)}) copy-start(bf16[256,512]{1,0:T(8,128)(2,1)} %param.11) | copy-start | bytes 786436
  38.3 25.3 %collective-permute-start.3 = (bf16[256,1024]{1,0:T(8,128)(2,1)S(1)}, bf16[256,1024]{1,0:T(8,128)(2,1)S(1)}, u32[]{:S(2)}, u32[]{:S(2)}) collective-permute-start(bf16[256,1024]{1,0:T(8,128)(2,1)S(1)} %maximum_select_fusion.1), channel_id=1, source_target_pairs={{0,6},{1,7},{2,0},{3,1},{4,2},{5,3},{6,4},{7,5},{8,14},{9,15},{10,... | collective-permute-start | bytes 1572872 | tf_op jit(solution)/shard_map/ppermute | solution.py:97
  41.4 22.2 %collective-permute-start.2 = (bf16[256,1024]{1,0:T(8,128)(2,1)S(1)}, bf16[256,1024]{1,0:T(8,128)(2,1)S(1)}, u32[]{:S(2)}, u32[]{:S(2)}) collective-permute-start(bf16[256,1024]{1,0:T(8,128)(2,1)S(1)} %maximum_select_fusion.1), channel_id=1, source_target_pairs={{0,4},{1,5},{2,6},{3,7},{4,0},{5,1},{6,2},{7,3},{8,12},{9,13},{10,... | collective-permute-start | bytes 1572872 | tf_op jit(solution)/shard_map/ppermute | solution.py:97
  42.0 25.2 %collective-permute-start.1 = (bf16[256,1024]{1,0:T(8,128)(2,1)S(1)}, bf16[256,1024]{1,0:T(8,128)(2,1)S(1)}, u32[]{:S(2)}, u32[]{:S(2)}) collective-permute-start(bf16[256,1024]{1,0:T(8,128)(2,1)S(1)} %maximum_select_fusion.1), channel_id=1, source_target_pairs={{0,2},{1,3},{2,4},{3,5},{4,6},{5,7},{6,0},{7,1},{8,10},{9,11},{10,... | collective-permute-start | bytes 1572872 | tf_op jit(solution)/shard_map/ppermute | solution.py:97
  81.8 4.4 %copy-start.4 = (bf16[256,4096]{1,0:T(8,128)(2,1)S(1)}, bf16[256,4096]{1,0:T(8,128)(2,1)}, u32[]{:S(2)}) copy-start(bf16[256,4096]{1,0:T(8,128)(2,1)} %copy.61) | copy-start | bytes 6291460
  81.8 4.4 %copy-start.6 = (bf16[256,4,1024]{0,2,1:T(8,128)(2,1)S(1)}, bf16[256,4,1024]{0,2,1:T(8,128)(2,1)}, u32[]{:S(2)}) copy-start(bf16[256,4,1024]{0,2,1:T(8,128)(2,1)} %copy.43) | copy-start | bytes 6291460
  87.1 34.9 %collective-permute-start.4 = (bf16[2,256,2,128]{1,3,2,0:T(8,128)(2,1)S(1)}, bf16[2,256,2,128]{1,3,2,0:T(8,128)(2,1)}, u32[]{:S(2)}, u32[]{:S(2)}) collective-permute-start(bf16[2,256,2,128]{1,3,2,0:T(8,128)(2,1)S(1)} %pad_maximum_fusion.2), channel_id=1, source_target_pairs={{0,32},{8,40},{16,48},{24,56},{32,64},{40,72},{48,80},{56,88},{64,... | collective-permute-start | bytes 786440 | tf_op jit(solution)/shard_map/ppermute | solution.py:145
  90.4 33.9 %collective-permute-start.5 = (bf16[2,256,2,128]{1,3,2,0:T(8,128)(2,1)S(1)}, bf16[2,256,2,128]{1,3,2,0:T(8,128)(2,1)}, u32[]{:S(2)}, u32[]{:S(2)}) collective-permute-start(bf16[2,256,2,128]{1,3,2,0:T(8,128)(2,1)S(1)} %pad_maximum_fusion.2), channel_id=1, source_target_pairs={{0,24},{8,32},{16,40},{24,48},{32,56},{40,64},{48,72},{56,80},{64,... | collective-permute-start | bytes 786440 | tf_op jit(solution)/shard_map/ppermute | solution.py:145
  92.7 32.6 %collective-permute-start.6 = (bf16[2,256,2,128]{1,3,2,0:T(8,128)(2,1)S(1)}, bf16[2,256,2,128]{1,3,2,0:T(8,128)(2,1)S(1)}, u32[]{:S(2)}, u32[]{:S(2)}) collective-permute-start(bf16[2,256,2,128]{1,3,2,0:T(8,128)(2,1)S(1)} %pad_maximum_fusion.2), channel_id=1, source_target_pairs={{0,16},{8,24},{16,32},{24,40},{32,48},{40,56},{48,64},{56,72},{64,... | collective-permute-start | bytes 786440 | tf_op jit(solution)/shard_map/ppermute | solution.py:145
  96.9 28.4 %copy-start.9 = (bf16[256,2,96]{0,2,1:T(8,128)(2,1)}, bf16[256,2,96]{0,2,1:T(8,128)(2,1)S(1)}, u32[]{:S(2)}) copy-start(bf16[256,2,96]{0,2,1:T(8,128)(2,1)S(1)} %slice.93) | copy-start | bytes 294916
  97.0 28.4 %collective-permute-start.7 = (bf16[2,256,2,128]{1,3,2,0:T(8,128)(2,1)S(1)}, bf16[2,256,2,128]{1,3,2,0:T(8,128)(2,1)S(1)}, u32[]{:S(2)}, u32[]{:S(2)}) collective-permute-start(bf16[2,256,2,128]{1,3,2,0:T(8,128)(2,1)S(1)} %pad_maximum_fusion.2), channel_id=1, source_target_pairs={{0,8},{8,16},{16,24},{24,32},{32,40},{40,48},{48,56},{56,64},{64,7... | collective-permute-start | bytes 786440 | tf_op jit(solution)/shard_map/ppermute | solution.py:145
  128.8 6.0 %copy-start.10 = (bf16[256,2,96]{0,2,1:T(8,128)(2,1)S(1)}, bf16[256,2,96]{0,2,1:T(8,128)(2,1)}, u32[]{:S(2)}) copy-start(bf16[256,2,96]{0,2,1:T(8,128)(2,1)} %copy-done.9) | copy-start | bytes 294916
  128.8 6.0 %copy-start.3 = (pred[256,8192]{1,0:T(8,128)(4,1)S(1)}, pred[256,8192]{1,0:T(8,128)(4,1)}, u32[]{:S(2)}) copy-start(pred[256,8192]{1,0:T(8,128)(4,1)} %broadcast_compare_fusion) | copy-start | bytes 6291460
  140.9 5.7 %copy-start.2 = (f32[2,256,8192]{2,1,0:T(8,128)}, f32[2,256,8192]{2,1,0:T(8,128)S(1)}, u32[]{:S(2)}) copy-start(f32[2,256,8192]{2,1,0:T(8,128)S(1)} %get-tuple-element.24) | copy-start | bytes 50331652
  146.6 9.5 %copy-start.7 = (f32[2,256,1280]{2,1,0:T(8,128)S(1)}, f32[2,256,1280]{2,1,0:T(8,128)}, u32[]{:S(2)}) copy-start(f32[2,256,1280]{2,1,0:T(8,128)} %get-tuple-element.26) | copy-start | bytes 7864324
  161.2 23.0 %collective-permute-start.10 = (bf16[64,4096]{1,0:T(8,128)(2,1)}, bf16[64,4096]{1,0:T(8,128)(2,1)}, u32[]{:S(2)}, u32[]{:S(2)}) collective-permute-start(bf16[64,4096]{1,0:T(8,128)(2,1)} %get-tuple-element.13), channel_id=1, source_target_pairs={{0,6},{1,7},{2,0},{3,1},{4,2},{5,3},{6,4},{7,5},{8,14},{9,15},{10,... | collective-permute-start | bytes 1572872 | tf_op jit(solution)/shard_map/ppermute | solution.py:184
  162.2 22.0 %collective-permute-start.9 = (bf16[64,4096]{1,0:T(8,128)(2,1)S(1)}, bf16[64,4096]{1,0:T(8,128)(2,1)}, u32[]{:S(2)}, u32[]{:S(2)}) collective-permute-start(bf16[64,4096]{1,0:T(8,128)(2,1)S(1)} %get-tuple-element.14), channel_id=1, source_target_pairs={{0,4},{1,5},{2,6},{3,7},{4,0},{5,1},{6,2},{7,3},{8,12},{9,13},{10,... | collective-permute-start | bytes 1572872 | tf_op jit(solution)/shard_map/ppermute | solution.py:184
  162.9 24.8 %collective-permute-start.8 = (bf16[64,4096]{1,0:T(8,128)(2,1)S(1)}, bf16[64,4096]{1,0:T(8,128)(2,1)}, u32[]{:S(2)}, u32[]{:S(2)}) collective-permute-start(bf16[64,4096]{1,0:T(8,128)(2,1)S(1)} %get-tuple-element.12), channel_id=1, source_target_pairs={{0,2},{1,3},{2,4},{3,5},{4,6},{5,7},{6,0},{7,1},{8,10},{9,11},{10,... | collective-permute-start | bytes 1572872 | tf_op jit(solution)/shard_map/ppermute | solution.py:184
  190.2 28.3 %collective-permute-start.11 = (f32[32,4096]{1,0:T(8,128)}, f32[32,4096]{1,0:T(8,128)}, u32[]{:S(2)}, u32[]{:S(2)}) collective-permute-start(f32[32,4096]{1,0:T(8,128)} %dynamic-slice_bitcast_fusion), channel_id=1, source_target_pairs={{0,1},{1,0},{2,3},{3,2},{4,5},{5,4},{6,7},{7,6},{8,9},{9,8},{10,11... | collective-permute-start | bytes 1572872 | tf_op jit(solution)/shard_map/ppermute | solution.py:190
  (4 other events, 6.2 us)
Sparse Core Ops, SparseCore 0:
  9.6 93.5 all-gather.1
